TPU v7x, 512 devices: a whole 4x4x16 slice. The times are simulated.
512 devices in a mesh: dp: 32 (over z, core), seq: 16 (over y, x).
Axes of the slice: x: 4, y: 4, z: 16, core: 2. Of those that a mesh axis runs over, the one named last changes fastest.
Arguments:
- mixer_in: bfloat16 [131072, 2816], P(('dp', 'seq')), parts along dimension 0, may hold values from -92 to 92
- gate_input: bfloat16 [131072, 2560], P(('dp', 'seq')), parts along dimension 0, may hold values from -6 to 6
- step_raw: bfloat16 [131072, 40], P(('dp', 'seq')), parts along dimension 0, may hold values from -6 to 6
- lengths: int32 [96], P('dp'), parts along dimension 0, may hold values from 1 to 2048, 4096 in all
- deal_order: int32 [512], P('dp'), parts along dimension 0, may hold values from 0 to 15, as said below
- conv_weight: float32 [4, 2816], replicated, may hold values from -3 to 3
- conv_bias: float32 [2816], replicated, may hold values from -3 to 3
- step_bias: float32 [40], replicated, may hold values from -4 to -1
- decay_rate: float32 [40], replicated, may hold values from 0.01 to 2
- skip_gain: float32 [40], replicated, may hold values from 0.5 to 1.5
- norm_gain: float32 [2560], replicated, may hold values from 0.5 to 1.5
Outputs:
- mixed_out: bfloat16 [131072, 2560], P(('dp', 'seq')), parts along dimension 0
- final_states: float32 [96, 2560, 128], P('dp', 'seq'), parts along dimension 0
There are 32 independent parts, one for each index of `dp`. A program takes and returns all parts, laid end to end along the dimension named above; an argument that names none is the same for every part. Nothing has to cross between parts.
Inputs may be any that keep to these rules, and one draw needn't show every extreme that they name: The prompt lengths sum to 4096 and the longest is exactly 2048. `deal_order`: every sequence stretch stands in exactly one dealt slot.
All inputs are finite; a program needn't handle non-finite values.
Results may differ from a plain program's by a relative error of at most 0.005.
Values may be sent and summed in bfloat16 or wider, within the bound.
No kernel may reach another device: no remote copies, remote signals or barrier semaphores. Data moves between devices by JAX's collectives and lax.ppermute only.
A program may use at most 128 MiB of HBM per device.

v0:
```python
import jax
import jax.numpy as jnp
from jax import lax
from jax.sharding import PartitionSpec as P

HEADS = 40
HEAD_DIM = 64
STATE = 128
KERNEL = 4
STRETCH = 256
DOCS = 3
INNER = 2560
CHANNELS = 2816


def doc_index(ends, positions):
    return jnp.sum((ends[None, :] <= positions[:, None]).astype(jnp.int32), axis=1)


def body(
    mixer_in,
    gate_input,
    step_raw,
    lengths,
    deal_order,
    conv_weight,
    conv_bias,
    step_bias,
    decay_rate,
    skip_gain,
    norm_gain,
):
    myself = lax.axis_index("seq")
    local_rows = mixer_in.shape[0]
    stretches_here = local_rows // STRETCH
    stretch_total = deal_order.shape[0]
    ends = jnp.cumsum(lengths)
    all_stretches = jnp.arange(stretch_total, dtype=jnp.int32)
    my_stretches = lax.dynamic_slice_in_dim(deal_order, myself * stretches_here, stretches_here)
    lane = jnp.arange(STRETCH, dtype=jnp.int32)
    own_doc = doc_index(
        ends, (my_stretches[:, None] * STRETCH + lane[None, :]).reshape(-1)
    ).reshape(stretches_here, STRETCH)
    prev_own = jnp.where(my_stretches > 0, doc_index(ends, my_stretches * STRETCH - 1), -1)
    blocks_in = mixer_in.reshape(stretches_here, STRETCH, CHANNELS)
    tails = blocks_in[:, STRETCH - (KERNEL - 1) :, :]
    step_blocks = step_raw.reshape(stretches_here, STRETCH, HEADS)
    step = jax.nn.softplus(step_blocks.astype(jnp.float32) + step_bias)
    log_decay = -decay_rate * step
    all_tails, all_steps = (
        lax.all_gather(tails, "seq", axis=0, tiled=True),
        lax.all_gather(step_blocks, "seq", axis=0, tiled=True),
    )
    totals = jnp.sum(
        -decay_rate * jax.nn.softplus(all_steps.astype(jnp.float32) + step_bias), axis=1
    )
    slot_map = (deal_order[:, None] == all_stretches[None, :]).astype(jnp.float32)
    packed_totals = jnp.dot(slot_map.T, totals, precision=lax.Precision.HIGHEST)
    prefix = jnp.cumsum(packed_totals, axis=0)
    base = jnp.concatenate([jnp.zeros((1, HEADS), jnp.float32), prefix[:-1]], 0)
    pick_own = (my_stretches[:, None] == all_stretches[None, :]).astype(jnp.float32)
    base_own = jnp.dot(pick_own, base, precision=lax.Precision.HIGHEST)
    running = base_own[:, None, :] + jnp.cumsum(log_decay, axis=1)
    prev_pick = (deal_order[None, :] == my_stretches[:, None] - 1).astype(jnp.bfloat16)
    prev_rows = jnp.einsum(
        "is,skc->ikc", prev_pick, all_tails, preferred_element_type=jnp.float32
    ).astype(jnp.bfloat16)
    extended = jnp.concatenate([prev_rows, blocks_in], 1)
    lead = (
        my_stretches[:, None] * STRETCH
        - (KERNEL - 1)
        + jnp.arange(KERNEL - 1, dtype=jnp.int32)[None, :]
    ).reshape(-1)
    ext_doc = jnp.concatenate(
        [doc_index(ends, lead).reshape(stretches_here, KERNEL - 1), own_doc], 1
    )
    accum = jnp.zeros((stretches_here, STRETCH, CHANNELS), jnp.float32) + conv_bias
    for offset in range(KERNEL):
        keep = (ext_doc[:, offset : offset + STRETCH] == own_doc).astype(jnp.float32)
        accum = (
            accum
            + conv_weight[offset]
            * extended[:, offset : offset + STRETCH, :].astype(jnp.float32)
            * keep[..., None]
        )
    mixed = jax.nn.silu(accum).astype(jnp.bfloat16)
    values = mixed[..., :INNER]
    input_map = mixed[..., INNER : INNER + STATE]
    output_map = mixed[..., INNER + STATE :]
    scaled = (values.astype(jnp.float32) * jnp.repeat(step, HEAD_DIM, axis=2)).astype(jnp.bfloat16)
    end_weight = jnp.exp(
        jnp.where((own_doc == own_doc[:, -1:])[..., None], running[:, -1:, :] - running, -jnp.inf)
    )
    weighted = (scaled.astype(jnp.float32) * jnp.repeat(end_weight, HEAD_DIM, axis=2)).astype(
        jnp.bfloat16
    )
    states = jnp.einsum("isk,isn->ikn", weighted, input_map, preferred_element_type=jnp.float32)
    source_pick = (deal_order[:, None] == all_stretches[None, :]).astype(jnp.float32)
    source_end = jnp.dot(source_pick, prefix, precision=lax.Precision.HIGHEST)
    source_doc = doc_index(ends, deal_order * STRETCH + STRETCH - 1)
    allowed = (deal_order[None, :] < my_stretches[:, None]) & (
        source_doc[None, :] == prev_own[:, None]
    )
    spans = jnp.exp(
        jnp.where(allowed[..., None], base_own[:, None, :] - source_end[None, :, :], -jnp.inf)
    )
    state_in = jnp.einsum(
        "ick,ckn->ikn",
        jnp.repeat(spans, HEAD_DIM, axis=2),
        lax.all_gather(states, "seq", axis=0, tiled=True),
        precision=lax.Precision.HIGHEST,
    )
    later = lane[:, None] >= lane[None, :]
    direct_gain = jnp.repeat(skip_gain, HEAD_DIM)[None, :]

    def stretch_out(inputs):
        values_c, scaled_c, keys_c, queries_c, running_c, doc_c, base_c, prev_c, state_c = inputs
        scores = jnp.dot(queries_c, keys_c.T, preferred_element_type=jnp.float32)
        same = (doc_c[:, None] == doc_c[None, :]) & later
        spans = running_c.T[:, :, None] - running_c.T[:, None, :]
        mixing = (scores[None] * jnp.exp(jnp.where(same[None], spans, -jnp.inf))).astype(
            jnp.bfloat16
        )
        within = jnp.einsum(
            "hts,shp->thp",
            mixing,
            scaled_c.reshape(STRETCH, HEADS, HEAD_DIM),
            preferred_element_type=jnp.float32,
        ).reshape(STRETCH, INNER)
        readout = jnp.dot(
            queries_c, state_c.astype(jnp.bfloat16).T, preferred_element_type=jnp.float32
        )
        carry_weight = jnp.exp(
            jnp.where((doc_c == prev_c)[:, None], running_c - base_c[None, :], -jnp.inf)
        )
        return (
            within
            + readout * jnp.repeat(carry_weight, HEAD_DIM, axis=1)
            + values_c.astype(jnp.float32) * direct_gain
        )

    outputs = lax.map(
        stretch_out,
        (values, scaled, input_map, output_map, running, own_doc, base_own, prev_own, state_in),
    )
    gated = outputs.reshape(local_rows, INNER) * jax.nn.silu(gate_input.astype(jnp.float32))
    normed = gated * lax.rsqrt(jnp.mean(gated * gated, axis=1, keepdims=True) + 1e-05) * norm_gain
    mixed_out = normed.astype(jnp.bfloat16)
    slot_numbers = jnp.arange(stretches_here, dtype=jnp.int32)

    def one_doc(document):
        last = lax.dynamic_index_in_dim(ends, document, keepdims=False) - 1
        owner = last // STRETCH
        match = my_stretches == owner
        slot = jnp.sum(jnp.where(match, slot_numbers, 0))

        def present():
            within_pos = last - owner * STRETCH
            running_c = lax.dynamic_index_in_dim(running, slot, keepdims=False)
            running_e = lax.dynamic_index_in_dim(running_c, within_pos, keepdims=False)
            doc_c = lax.dynamic_index_in_dim(own_doc, slot, keepdims=False)
            scaled_c = lax.dynamic_index_in_dim(scaled, slot, keepdims=False)
            keys_c = lax.dynamic_index_in_dim(input_map, slot, keepdims=False)
            base_c = lax.dynamic_index_in_dim(base_own, slot, keepdims=False)
            prev_c = lax.dynamic_index_in_dim(prev_own, slot, keepdims=False)
            state_c = lax.dynamic_index_in_dim(state_in, slot, keepdims=False)
            weight = jnp.exp(
                jnp.where((doc_c == document)[:, None], running_e[None, :] - running_c, -jnp.inf)
            )
            final_weighted = (
                scaled_c.astype(jnp.float32) * jnp.repeat(weight, HEAD_DIM, axis=1)
            ).astype(jnp.bfloat16)
            part = jnp.dot(final_weighted.T, keys_c, preferred_element_type=jnp.float32)
            carry_weight = jnp.exp(jnp.where(prev_c == document, running_e - base_c, -jnp.inf))
            return part + jnp.repeat(carry_weight, HEAD_DIM)[:, None] * state_c

        def absent():
            return jnp.zeros((INNER, STATE), jnp.float32)

        return lax.cond(jnp.any(match), present, absent)

    every_doc = jnp.transpose(lax.map(one_doc, jnp.arange(DOCS, dtype=jnp.int32)), (1, 0, 2))
    kept = lax.psum_scatter(
        every_doc.astype(jnp.bfloat16), "seq", scatter_dimension=0, tiled=True
    ).astype(jnp.float32)
    final_states = jnp.transpose(kept, (1, 0, 2))
    return (mixed_out, final_states)


def solution(mesh):
    return jax.shard_map(
        body,
        mesh=mesh,
        in_specs=(
            P(("dp", "seq"), None),
            P(("dp", "seq"), None),
            P(("dp", "seq"), None),
            P("dp"),
            P("dp"),
            P(),
            P(),
            P(),
            P(),
            P(),
            P(),
        ),
        out_specs=(P(("dp", "seq"), None), P("dp", "seq", None)),
        check_vma=False,
    )
```

profile of v0, /device:TPU:1, one launch (start us, length us, event | category | flops | bytes accessed | tf_op | source)
XLA Modules:
  0.0 391.2 jit_solution(15185379277083827339)
XLA Ops:
  7.9 20.5 %all-gather = bf16[4096,40]{0,1:T(8,128)(2,1)S(1)} all-gather(bf16[256,40]{0,1:T(8,128)(2,1)} %param.17), channel_id=2, replica_groups=mesh['dp'=32,'seq'=16] {'seq'}, dimensions={0}, use_global_device_ids=true | all-gather | bytes 348160 | tf_op jit(solution)/shard_map/all_gather | solution.py:52
  28.4 0.8 multiply_bitcast_fusion
  30.0 1.2 dynamic_slice.62
  32.6 0.8 reduce-window.10
  34.4 0.8 slice.76
  35.2 17.4 %all_gather.9 = bf16[16,3,2816]{2,1,0:T(4,128)(2,1)S(1)} all-gather(bf16[1,3,2816]{2,1,0:T(4,128)(2,1)S(1)} %slice.76), channel_id=1, replica_groups=mesh['dp'=32,'seq'=16] {'seq'}, dimensions={0}, use_global_device_ids=true | all-gather | bytes 287232 | tf_op jit(solution)/shard_map/all_gather | solution.py:51
  52.6 0.8 fusion.32
  53.4 1.1 slice_reduce_fusion.5
  54.7 2.1 copy.73
  59.4 0.8 fusion.42
  62.7 2.1 copy.78
  64.8 5.9 %multiply_convert_fusion.2 = bf16[1,256,2816]{2,1,0:T(8,128)(2,1)S(1)} fusion(bf16[256,2816]{1,0:T(8,128)(2,1)} %param.15, bf16[1,3,2816]{2,1,0:T(4,128)(2,1)S(1)} %copy.108, bf16[1,256,2816]{2,1,0:T(8,128)(2,1)} %bitcast.153, f32[2816]{0:T(1024)S(1)} %get-tuple-element.357, f32[256]{0:T(256)S(1)} %bitcast.173, f32[2816]{0:T(1024)S(1)} %get-tuple-element.358, ...), kind=kLoop, calls=%fused_computation.33 | loop fusion | flops 20905984 | bytes 4401664 | tf_op jit(solution)/shard_map/convert_element_type | solution.py:86
  71.1 1.9 copy-done.1
  73.0 1.8 fusion.25
  75.1 1.4 copy.74
  77.6 157.3 %all-gather.4.cloned.1.call-done = f32[40960,128]{1,0:T(8,128)} async-done(((f32[2560,128]{1,0:T(8,128)}), f32[40960,128]{1,0:T(8,128)}) %all-gather.4.cloned.1.call-update) | async-done | bytes 20971536 | tf_op jit(solution)/shard_map/all_gather | solution.py:110
  235.0 38.9 %fusion.6 = f32[2560,1,128]{2,1,0:T(1,128)S(1)} fusion(f32[16,2560,1]{0,2,1:T(1,128)S(1)} %bitcast.151, f32[16,2560,128]{2,1,0:T(8,128)} %bitcast.147), kind=kOutput, calls=%fused_computation.15 | convolution fusion | flops 62914560 | bytes 22446080 | tf_op jit(solution)/shard_map/ick,ckn->ikn/dot_general | solution.py:107
  273.9 20.2 %while.17 = (s32[]{:T(128)}, bf16[3,2560,128]{2,1,0:T(8,128)(2,1)}, s32[3]{0:T(128)S(1)}, s32[3]{0:T(128)S(1)}, s32[1]{0:T(128)}, /*index=5*/bf16[1,256,2560]{1,...) while((s32[]{:T(128)}, bf16[3,2560,128]{2,1,0:T(8,128)(2,1)}, ...), condition=%wide.region_13.14_spmd, body=%wide.region_10.13_spmd.sunk | while | flops 170742112 | bytes 7442075 | solution.py:182
  278.4 4.0 %conditional.2 = (bf16[1,2560,128]{2,1,0:T(8,128)(2,1)S(1)}) conditional(s32[]{:T(128)} %bitcast.143, () %tuple.66, (bf16[1,256,2560]{1,2,0:T(8,128)(2,1)}, s32[]{:T(128)}, s32[1,256]{1,0:T(1,128)S(1)}, s32[]{:T(128)}, s32[]{:T(128)}, /*index=5*/f32[1,256,40]{1,2,0:T(8,128)S(1)}, bf16[1,256,128]{2,1,0:T(8,128)(2,1)S(1)}, s32[1]{0:T(128)}, ...), branch_computations={%region_11.11_spmd, %region_12.12_spmd} | conditional | flops 170742096 | bytes 6130356 | solution.py:180
  279.3 1.7 fusion.1
  282.3 0.9 constant_dynamic-update-slice_fusion.2
  287.7 0.9 constant_dynamic-update-slice_fusion.2
  293.2 0.9 constant_dynamic-update-slice_fusion.2
  294.2 1.1 fusion.36
  295.3 5.1 %fusion.8 = f32[40,64,256]{2,1,0:T(8,128)} fusion(bf16[256,40,64]{0,2,1:T(8,128)(2,1)} %bitcast.28, f32[40,256]{1,0:T(8,128)S(1)} %bitcast.154, f32[256,256]{1,0:T(8,128)S(1)} %fusion.36, pred[256,256]{1,0:T(8,128)(4,1)S(1)} %fusion.34), kind=kOutput, calls=%fused_computation.18 | convolution fusion | flops 346030080 | bytes 4300800 | tf_op jit(solution)/shard_map/while/body/eval_jaxpr/hts,shp->thp/dot_general | solution.py:124
  300.4 3.2 copy.80
  303.7 1.7 broadcast_in_dim.192
  305.4 3.4 copy.79
  308.9 4.6 %multiply_reduce_fusion = (f32[256]{0:T(256)S(1)}, f32[256,2560]{1,0:T(8,128)S(1)}) fusion(bf16[256,2560]{1,0:T(8,128)(2,1)S(1)} %copy-done.8, f32[2560]{0:T(1024)S(1)} %mul.239, bf16[1,256,2816]{2,1,0:T(8,128)(2,1)} %copy-done.2, f32[256,2560]{1,0:T(8,128)} %copy.80, f32[256,2560]{1,0:T(8,128)} %copy.79, f32[2560,128]{1,0:T(8,128)S(1)} %bitcast.146), kind=kOutput, calls=%fused_computation.40 | convolution fusion | flops 176619264 | bytes 11873280 | tf_op jit(solution)/shard_map/while/body/eval_jaxpr/dot_general | solution.py:130
  313.5 1.3 multiply_convert_fusion.3
  314.9 67.9 %reduce-scatter.2.cloned.1.call-done = bf16[160,3,128]{2,0,1:T(8,128)(2,1)} async-done(((bf16[2560,3,128]{2,0,1:T(8,128)(2,1)}), bf16[160,3,128]{2,0,1:T(8,128)(2,1)}) %reduce-scatter.2.cloned.1.call-update) | async-done | bytes 122896 | tf_op jit(solution)/shard_map/reduce_scatter | solution.py:183
  382.7 1.6 convert_bitcast_fusion.2
  (83 shorter events, 14.1 us)
Async XLA Ops:
  7.2 227.8 %all-gather.4.cloned.1.call-start = ((), (), s32[]{:S(2)}) async-start(), calls=%async_computation.2 | async-start | bytes 22282240 | tf_op jit(solution)/shard_map/all_gather | solution.py:110
  54.7 3.7 copy-start.6
  56.8 2.1 copy-start.5
  62.7 2.1 copy-start.4
  64.8 5.9 %copy-start = (f32[1,256,2560]{2,1,0:T(8,128)S(1)}, f32[1,256,2560]{2,1,0:T(8,128)}, u32[]{:S(2)}) copy-start(f32[1,256,2560]{2,1,0:T(8,128)} %copy.73) | copy-start | bytes 7864324
  70.7 164.3 %copy-start.2 = (bf16[1,256,2816]{2,1,0:T(8,128)(2,1)}, bf16[1,256,2816]{2,1,0:T(8,128)(2,1)S(1)}, u32[]{:S(2)}) copy-start(bf16[1,256,2816]{2,1,0:T(8,128)(2,1)S(1)} %multiply_convert_fusion.2) | copy-start | bytes 4325380
  70.7 2.3 copy-start.1
  74.9 307.9 %reduce-scatter.2.cloned.1.call-start = ((), (), s32[]{:S(2)}) async-start(), calls=%async_computation.1 | async-start | bytes 2088960 | tf_op jit(solution)/shard_map/reduce_scatter | solution.py:183
  305.4 3.4 copy-start.7
  305.4 3.5 copy-start.8
  308.9 4.6 %copy-start.3 = (f32[2560]{0:T(1024)S(1)}, f32[2560]{0:T(1024)}, u32[]{:S(2)}) copy-start(f32[2560]{0:T(1024)} %param.25) | copy-start | bytes 30724
Sparse Core Ops, SparseCore 0:
  75.0 159.8 all-gather.3
  294.2 88.4 reduce-scatter.1
where the time goes:
time: 393 us; the launch traced here: 391 us
  waiting for transfers between devices  225 us (57%)
  matrix products  54 us (14%)
  blocking collectives  37.9 us (10%)
  local copies, waits for them, and re-layouts  28.5 us (7%)
  other arithmetic  18 us (5%)
  between operations  17 us (4%)
  loops' own time  10.3 us (3%)
    all_gather x1, waiting for transfers between devices, body(): lax.all_gather(states, 'seq', axis=0, tiled=True)  157 us
    reduce_scatter x1, waiting for transfers between devices, body(): lax.psum_scatter(every_doc.astype(jnp.bfloat16), 'seq', scatter_dimension...  67.9 us
    dot_general x1, matrix products, body(): jnp.einsum('ick,ckn->ikn', jnp.repeat(spans, HEAD_DIM, axis=2), lax.all_g...  38.9 us
    all_gather x1, blocking collectives, body(): lax.all_gather(step_blocks, 'seq', axis=0, tiled=True)  20.5 us
    all_gather x1, blocking collectives, body(): lax.all_gather(tails, 'seq', axis=0, tiled=True)  17.4 us
    another operation x1, loops' own time, body(): lax.map(one_doc, jnp.arange(DOCS, dtype=jnp.int32))  9.57 us
  transfers between devices with their start and end apart: 2, of which 2 were waited for; matrix products, arithmetic and copies ran while one was open for 6% of the time, Pallas kernels for 0%

commit v1 on v0

v1 whole, which is shorter than its diff:
```python
import jax
import jax.numpy as jnp
from jax import lax
from jax.sharding import PartitionSpec as P

HEADS = 40
HEAD_DIM = 64
STATE = 128
KERNEL = 4
STRETCH = 256
INNER = 2560
CHANNELS = 2816
LEAD = KERNEL - 1
FINAL_VIA_ALL_TO_ALL = True

f32 = jnp.float32
bf16 = jnp.bfloat16


def doc_index(ends, positions):
    return jnp.sum((ends[None, :] <= positions[..., None]).astype(jnp.int32), axis=-1)


def per_head(x):
    return jnp.repeat(x, HEAD_DIM, axis=-1)


def conv_rows(ext, ext_doc, out_doc, conv_weight, conv_bias):
    rows = out_doc.shape[-1]
    accum = jnp.zeros(ext.shape[:-2] + (rows, CHANNELS), f32) + conv_bias
    for offset in range(KERNEL):
        keep = (ext_doc[..., offset : offset + rows] == out_doc).astype(f32)
        accum = (
            accum
            + conv_weight[offset]
            * ext[..., offset : offset + rows, :].astype(f32)
            * keep[..., None]
        )
    return jax.nn.silu(accum).astype(bf16)


def body(
    mixer_in,
    gate_input,
    step_raw,
    lengths,
    deal_order,
    conv_weight,
    conv_bias,
    step_bias,
    decay_rate,
    skip_gain,
    norm_gain,
):
    n = deal_order.shape[0]
    docs = lengths.shape[0]
    me = lax.axis_index("seq")
    rows_here = INNER // n
    mine = deal_order[me]
    ends = jnp.cumsum(lengths).astype(jnp.int32)
    lane = jnp.arange(STRETCH, dtype=jnp.int32)
    doc = doc_index(ends, mine * STRETCH + lane)
    end_doc_mine = doc[-1]

    step = jax.nn.softplus(step_raw.astype(f32) + step_bias)
    log_decay = -decay_rate * step
    lc = jnp.cumsum(log_decay, axis=0)
    total = lc[-1]

    ext_local = jnp.concatenate([jnp.zeros((LEAD, CHANNELS), bf16), mixer_in], 0)
    ext_doc_local = jnp.concatenate([jnp.full((LEAD,), -1, jnp.int32), doc], 0)
    mixed_local = conv_rows(ext_local, ext_doc_local, doc, conv_weight, conv_bias)
    scaled_local = (
        mixed_local[:, :INNER].astype(f32) * per_head(step)
    ).astype(bf16)
    keys_local = mixed_local[:, INNER : INNER + STATE]
    weight_end = jnp.where(
        ((doc == end_doc_mine) & (lane >= LEAD))[:, None], jnp.exp(total[None, :] - lc), 0.0
    )
    weighted_local = (scaled_local.astype(f32) * per_head(weight_end)).astype(bf16)
    state_part = jnp.dot(weighted_local.T, keys_local, preferred_element_type=f32)
    gathered_states = lax.all_gather(state_part.astype(bf16), "seq", axis=0, tiled=False)

    doc_last = ends - 1
    doc_owner = doc_last // STRETCH
    doc_at = doc_last - doc_owner * STRETCH
    lc_at_end = jnp.where(
        (doc_owner == mine)[:, None], lc[jnp.clip(doc_at, 0, STRETCH - 1)], 0.0
    )
    w_lead = jnp.where(
        (doc[:LEAD] == end_doc_mine)[:, None], jnp.exp(total[None, :] - lc[:LEAD]), 0.0
    )
    edge_rows = jnp.concatenate([mixer_in[:LEAD], mixer_in[STRETCH - LEAD :]], 0).astype(f32)
    pieces = [
        edge_rows.reshape(-1),
        total,
        step[:LEAD].reshape(-1),
        w_lead.reshape(-1),
        lc_at_end.reshape(-1),
    ]
    flat = jnp.concatenate(pieces)
    width = flat.shape[0]
    padded_width = -(-width // 128) * 128
    flat = jnp.pad(flat, (0, padded_width - width))
    small = lax.all_gather(flat, "seq", axis=0, tiled=False)

    slots = jnp.arange(n, dtype=jnp.int32)
    holder = jnp.sum(
        jnp.where(deal_order[None, :] == slots[:, None], slots[None, :], 0), axis=1
    )
    seq_small = jnp.take(small, holder, axis=0)
    cursor = 0
    sizes = [2 * LEAD * CHANNELS, HEADS, LEAD * HEADS, LEAD * HEADS, docs * HEADS]
    cut = []
    for size in sizes:
        cut.append((cursor, cursor + size))
        cursor += size
    edge_seq = seq_small[:, cut[0][0] : cut[0][1]].reshape(n, 2 * LEAD, CHANNELS)
    totals_seq = seq_small[:, cut[1][0] : cut[1][1]]
    step_lead_seq = seq_small[:, cut[2][0] : cut[2][1]].reshape(n, LEAD, HEADS)
    w_lead_seq = seq_small[:, cut[3][0] : cut[3][1]].reshape(n, LEAD, HEADS)
    lc_end = jnp.sum(small[:, cut[4][0] : cut[4][1]], axis=0).reshape(docs, HEADS)

    head_seq = edge_seq[:, :LEAD].astype(bf16)
    tail_seq = edge_seq[:, LEAD:].astype(bf16)
    prev_tail = jnp.concatenate([jnp.zeros((1, LEAD, CHANNELS), bf16), tail_seq[:-1]], 0)
    ext6 = jnp.concatenate([prev_tail, head_seq], 1)
    ext6_pos = slots[:, None] * STRETCH - LEAD + jnp.arange(2 * LEAD, dtype=jnp.int32)[None, :]
    ext6_doc = jnp.where(ext6_pos >= 0, doc_index(ends, ext6_pos), -1)
    lead_doc = ext6_doc[:, LEAD:]
    mixed_lead = conv_rows(ext6, ext6_doc, lead_doc, conv_weight, conv_bias)
    scaled_lead = (mixed_lead[..., :INNER].astype(f32) * per_head(step_lead_seq)).astype(bf16)
    keys_lead = mixed_lead[..., INNER : INNER + STATE]
    weighted_lead = (scaled_lead.astype(f32) * per_head(w_lead_seq)).astype(bf16)

    mixed = jnp.concatenate([mixed_lead[mine], mixed_local[LEAD:]], 0)
    values = mixed[:, :INNER]
    keys = mixed[:, INNER : INNER + STATE]
    queries = mixed[:, INNER + STATE :]
    scaled = (values.astype(f32) * per_head(step)).astype(bf16)

    end_doc_seq = doc_index(ends, slots * STRETCH + STRETCH - 1)
    prev_seq = jnp.where(slots > 0, doc_index(ends, slots * STRETCH - 1), -1)
    between = (slots[None, :, None] < slots[None, None, :]) & (
        slots[None, None, :] < slots[:, None, None]
    )
    gap = jnp.sum(jnp.where(between[..., None], totals_seq[None, None], 0.0), axis=2)
    allowed = (slots[None, :] < slots[:, None]) & (end_doc_seq[None, :] == prev_seq[:, None])
    cross = jnp.where(allowed[..., None], jnp.exp(gap), 0.0)
    cross_dev = jnp.take(cross, deal_order, axis=1)

    receivers = jnp.concatenate([mine[None], doc_owner])
    recv_cross = cross[receivers]
    lead_mix = (
        per_head(recv_cross)[:, :, None, :] * weighted_lead.astype(f32)[None]
    ).reshape(receivers.shape[0], n * LEAD, INNER)
    lead_state = jnp.einsum(
        "rxk,xn->rkn",
        lead_mix,
        keys_lead.reshape(n * LEAD, STATE).astype(f32),
        precision=lax.Precision.HIGHEST,
    )

    scores = jnp.dot(queries, keys.T, preferred_element_type=f32)
    later = lane[:, None] >= lane[None, :]
    same = (doc[:, None] == doc[None, :]) & later
    spans = lc.T[:, :, None] - lc.T[:, None, :]
    mixing = (scores[None] * jnp.exp(jnp.where(same[None], spans, -jnp.inf))).astype(bf16)
    within = jnp.einsum(
        "hts,shp->thp",
        mixing,
        scaled.reshape(STRETCH, HEADS, HEAD_DIM),
        preferred_element_type=f32,
    ).reshape(STRETCH, INNER)
    direct = values.astype(f32) * per_head(skip_gain)[None, :]

    doc_ids = jnp.arange(docs, dtype=jnp.int32)
    lc_own_end = lc[jnp.clip(doc_at, 0, STRETCH - 1)]
    final_weight = jnp.where(
        ((doc[None, :] == doc_ids[:, None]) & (doc_owner == mine)[:, None])[..., None],
        jnp.exp(lc_own_end[:, None, :] - lc[None]),
        0.0,
    )
    final_weighted = (scaled.astype(f32)[None] * per_head(final_weight)).astype(bf16)
    final_part = jnp.einsum(
        "dsk,sn->dkn", final_weighted, keys, preferred_element_type=f32
    ).astype(bf16)
    if FINAL_VIA_ALL_TO_ALL:
        parts_in = lax.all_to_all(
            final_part.reshape(docs, n, rows_here, STATE), "seq", 1, 1, tiled=True
        )
        part_here = jnp.sum(parts_in.astype(f32), axis=1)
    else:
        part_here = jnp.transpose(
            lax.psum_scatter(
                jnp.transpose(final_part, (1, 0, 2)), "seq", scatter_dimension=0, tiled=True
            ),
            (1, 0, 2),
        ).astype(f32)

    gs = gathered_states.astype(f32)
    state_in = (
        jnp.sum(
            cross_dev[mine][:, :, None, None]
            * gs.reshape(n, HEADS, HEAD_DIM, STATE),
            axis=0,
        ).reshape(INNER, STATE)
        + lead_state[0]
    )
    readout = jnp.dot(queries, state_in.astype(bf16).T, preferred_element_type=f32)
    carry_weight = jnp.exp(jnp.where((doc == prev_seq[mine])[:, None], lc, -jnp.inf))
    outputs = within + readout * per_head(carry_weight) + direct
    gated = outputs * jax.nn.silu(gate_input.astype(f32))
    normed = gated * lax.rsqrt(jnp.mean(gated * gated, axis=1, keepdims=True) + 1e-05) * norm_gain
    mixed_out = normed.astype(bf16)

    row_ids = me * rows_here + jnp.arange(rows_here, dtype=jnp.int32)
    row_head = row_ids // HEAD_DIM
    gs_rows = lax.dynamic_slice_in_dim(gs, me * rows_here, rows_here, axis=1)
    owner_cross = cross_dev[doc_owner][:, :, row_head]
    owner_in = jnp.einsum("dkr,krn->drn", owner_cross, gs_rows, precision=lax.Precision.HIGHEST)
    owner_in = owner_in + lax.dynamic_slice_in_dim(lead_state[1:], me * rows_here, rows_here, axis=1)
    carry_final = jnp.where(
        (prev_seq[doc_owner] == doc_ids)[:, None], jnp.exp(lc_end[:, row_head]), 0.0
    )
    final_states = part_here + carry_final[..., None] * owner_in
    return (mixed_out, final_states)


def solution(mesh):
    return jax.shard_map(
        body,
        mesh=mesh,
        in_specs=(
            P(("dp", "seq"), None),
            P(("dp", "seq"), None),
            P(("dp", "seq"), None),
            P("dp"),
            P("dp"),
            P(),
            P(),
            P(),
            P(),
            P(),
            P(),
        ),
        out_specs=(P(("dp", "seq"), None), P("dp", "seq", None)),
        check_vma=False,
    )
```

time: 393 us -> 225 us (0.57)
  waiting for transfers between devices: 225 us -> 92.7 us
  matrix products: 54 us -> 14.7 us
  blocking collectives: 37.9 us -> 0 us
  local copies, waits for them, and re-layouts: 28.5 us -> 54.7 us
  other arithmetic: 18 us -> 39.2 us
  loops' own time: 10.3 us -> 0 us
  starting transfers between devices: 0.26 us -> 5.24 us
    all_gather x1 -> x2, waiting for transfers between devices: 157 us -> 89.4 us  [the longest x1 57 us: body(): lax.all_gather(state_part.astype(bf16), 'seq', axis=0, tiled=False)]
    reduce_scatter x1 -> x0, waiting for transfers between devices: 67.9 us -> none  [body(): lax.psum_scatter(every_doc.astype(jnp.bfloat16), 'seq', scatter_dimension...]
    dot_general x10 -> x7, matrix products: 54 us -> 14.7 us  [the longest x1 4.85 us: body(): jnp.einsum('hts,shp->thp', mixing, scaled.reshape(STRETCH, HEADS, HEAD_DI...]
    all_gather x2 -> x0, blocking collectives: 37.9 us -> none  [the longest x1 20.5 us: body(): lax.all_gather(step_blocks, 'seq', axis=0, tiled=True)]
    reduce_sum x5 -> x8, other arithmetic: 1.56 us -> 15.9 us  [the longest x1 12.7 us: body(): jnp.sum(cross_dev[mine][:, :, None, None] * gs.reshape(n, HEADS, HEAD_DIM...]
    another operation x4 -> x0, loops' own time: 10.3 us -> none  [the longest x1 9.57 us: body(): lax.map(one_doc, jnp.arange(DOCS, dtype=jnp.int32))]
    gather x0 -> x10, local copies, waits for them, and re-layouts: none -> 8.07 us  [the longest x3 2.21 us: body(): owner_cross = cross_dev[doc_owner][:, :, row_head]]
    reshape x2 -> x16, local copies, waits for them, and re-layouts: 6.58 us -> 13.2 us  [the longest x5 7.99 us: per_head(): return jnp.repeat(x, HEAD_DIM, axis=-1)]
  transfers between devices with their start and end apart: 2 -> 3, of which waited for: 2 -> 3; matrix products, arithmetic and copies ran while one was open for 6% -> 33% of each run, Pallas kernels for 0% -> 0%
where the time goes in v1:
time: 225 us; the launch traced here: 224 us
  waiting for transfers between devices  92.7 us (41%)
  local copies, waits for them, and re-layouts  54.7 us (24%)
  other arithmetic  39.2 us (17%)
  between operations  17.4 us (8%)
  matrix products  14.7 us (7%)
  starting transfers between devices  5.24 us (2%)
    all_gather x1, waiting for transfers between devices, body(): lax.all_gather(state_part.astype(bf16), 'seq', axis=0, tiled=False)  57 us
    all_gather x1, waiting for transfers between devices, body(): small = lax.all_gather(flat, 'seq', axis=0, tiled=False)  32.4 us
    reduce_sum x1, other arithmetic, body(): jnp.sum(cross_dev[mine][:, :, None, None] * gs.reshape(n, HEADS, HEAD_DIM...  12.7 us
    reshape x5, local copies, waits for them, and re-layouts, per_head(): return jnp.repeat(x, HEAD_DIM, axis=-1)  7.99 us
    convert_element_type x2, other arithmetic, conv_rows(): return jax.nn.silu(accum).astype(bf16)  6.24 us
    broadcast_in_dim x7, local copies, waits for them, and re-layouts, per_head(): return jnp.repeat(x, HEAD_DIM, axis=-1)  5.77 us
    unnamed x50, local copies, waits for them, and re-layouts  5.4 us
    all_to_all x1, starting transfers between devices, body(): lax.all_to_all(final_part.reshape(docs, n, rows_here, STATE), 'seq', 1, 1...  5.16 us
  transfers between devices with their start and end apart: 3, of which 3 were waited for; matrix products, arithmetic and copies ran while one was open for 33% of the time, Pallas kernels for 0%

profile of v1, /device:TPU:1, one launch (start us, length us, event | category | flops | bytes accessed | tf_op | source)
XLA Modules:
  0.0 223.8 jit_solution(16482531194283813111)
XLA Ops:
  23.3 2.1 copy.183
  25.4 1.7 broadcast_in_dim.248
  27.1 2.2 copy.178
  29.4 5.9 %multiply_convert_fusion.2 = bf16[256,2816]{1,0:T(8,128)(2,1)S(1)} fusion(bf16[256,2816]{1,0:T(8,128)(2,1)} %param.11, f32[2816]{0:T(1024)S(1)} %get-tuple-element.4, f32[256]{0:T(256)S(1)} %get-tuple-element.26, f32[2816]{0:T(1024)S(1)} %get-tuple-element.5, f32[256]{0:T(256)S(1)} %get-tuple-element.27, f32[2816]{0:T(1024)S(1)} %get-tuple-element.3, ...), kind=kLoop, calls=%fused_computation.30 | loop fusion | flops 14417920 | bytes 2942976 | tf_op jit(solution)/shard_map/convert_element_type | solution.py:39
  36.4 1.6 convolution_convert_fusion.1
  38.0 1.7 slice.202
  40.6 1.7 broadcast_in_dim.267
  42.3 3.2 %copy.187 = f32[256,2560]{1,0:T(8,128)} copy(f32[256,2560]{0,1:T(8,128)} %bitcast.110) | data formatting | bytes 5242880 | tf_op jit(solution)/shard_map/reshape | solution.py:25
  47.6 32.4 %all-gather.5.cloned.1.call-done = f32[278528]{0:T(1024)} async-done(((f32[17408]{0:T(1024)}), f32[278528]{0:T(1024)}) %all-gather.5.cloned.1.call-update) | async-done | bytes 1114128 | tf_op jit(solution)/shard_map/all_gather | solution.py:105
  80.0 1.4 reshape.680
  81.5 1.8 gather_fusion.1
  83.3 1.4 broadcast_select_fusion
  86.5 1.9 reshape.615
  90.1 1.5 fusion.10
  91.6 2.4 %copy.179 = bf16[256,2560]{0,1:T(8,128)(2,1)} copy(bf16[256,2560]{1,0:T(8,128)(2,1)} %fusion.10) | data formatting | bytes 2621440 | tf_op jit(solution)/shard_map/convert_element_type | solution.py:140
  94.1 2.9 %copy.189 = f32[256,2560]{0,1:T(8,128)} copy(bf16[256,2560]{1,0:T(8,128)(2,1)} %fusion.10) | data formatting | bytes 3932160 | tf_op jit(solution)/shard_map/convert_element_type | solution.py:184
  102.2 1.6 gather_fusion.7
  103.7 2.5 %fusion = bf16[3,256,2560]{1,2,0:T(8,128)(2,1)S(1)} fusion(f32[3,256,40]{1,2,0:T(8,128)S(1)} %exponential_select_fusion, f32[256,2560]{0,1:T(8,128)} %copy.189), kind=kLoop, calls=%fused_computation.11 | loop fusion | flops 3932160 | bytes 6676480 | tf_op jit(solution)/shard_map/convert_element_type | solution.py:184
  107.4 1.4 copy.190
  108.8 5.2 %all-to-all-start = ((bf16[3,16,160,128]{3,2,0,1:T(8,128)(2,1)}), bf16[3,16,160,128]{3,2,0,1:T(8,128)(2,1)}, u32[]{:S(2)}, u32[]{:S(2)}) async-start(bf16[3,16,160,128]{3,2,0,1:T(8,128)(2,1)} %copy.190), calls=%async_computation | async-start | bytes 3932160 | tf_op jit(solution)/shard_map/all_to_all | solution.py:189
  116.3 1.5 gather_fusion.3
  117.8 1.5 broadcast_in_dim.262
  119.2 1.6 mul.340
  121.1 4.9 %fusion.1 = f32[40,64,256]{2,1,0:T(8,128)} fusion(bf16[256,40,64]{0,2,1:T(8,128)(2,1)} %bitcast.112, f32[40,256]{1,0:T(8,128)} %get-tuple-element.18, f32[256,256]{1,0:T(8,128)S(1)} %fusion.50, pred[256,256]{1,0:T(8,128)(4,1)S(1)} %copy-done.14), kind=kOutput, calls=%fused_computation.12 | convolution fusion | flops 346030080 | bytes 4300800 | tf_op jit(solution)/shard_map/hts,shp->thp/dot_general | solution.py:169
  125.9 3.2 %copy.188 = f32[256,2560]{1,0:T(8,128)} copy(f32[256,2560]{0,1:T(8,128)} %bitcast.111) | data formatting | bytes 5242880 | tf_op jit(solution)/shard_map/reshape | solution.py:174
  129.2 4.3 %convolution_bitcast_fusion = f32[4,2560,128]{2,1,0:T(8,128)S(1)} fusion(f32[16,3,2560]{2,0,1:T(8,128)S(1)} %fusion.27, f32[4,16,2560]{2,1,0:T(8,128)S(1)} %mul.340, bf16[16,3,2816]{2,0,1:T(8,128)(2,1)S(1)} %copy-done.9), kind=kOutput, calls=%fused_computation.18 | convolution fusion | flops 755466240 | bytes 6402048 | tf_op jit(solution)/shard_map/rxk,xn->rkn/dot_general | solution.py:157
  133.5 2.4 %copy-done.2 = f32[4,2560,128]{2,1,0:T(8,128)} copy-done((f32[4,2560,128]{2,1,0:T(8,128)}, f32[4,2560,128]{2,1,0:T(8,128)S(1)}, u32[]{:S(2)}) %copy-start.2) | copy-done | bytes 5242904
  135.9 3.2 %all-to-all-done = bf16[3,16,160,128]{3,2,0,1:T(8,128)(2,1)} async-done(((bf16[3,16,160,128]{3,2,0,1:T(8,128)(2,1)}), bf16[3,16,160,128]{3,2,0,1:T(8,128)(2,1)}, u32[]{:S(2)}, u32[]{:S(2)}) %all-to-all-start) | async-done | bytes 1966112 | tf_op jit(solution)/shard_map/all_to_all | solution.py:189
  139.1 1.8 convert_reduce_fusion
  140.9 57.0 %all-gather.7.cloned.1.call-done = bf16[40960,128]{1,0:T(8,128)(2,1)} async-done(((bf16[2560,128]{1,0:T(8,128)(2,1)}), bf16[40960,128]{1,0:T(8,128)(2,1)}) %all-gather.7.cloned.1.call-update) | async-done | bytes 10485776 | tf_op jit(solution)/shard_map/all_gather | solution.py:82
  199.3 12.7 %multiply_reduce_fusion = f32[2560,128]{1,0:T(8,128)S(1)} fusion(bf16[16,2560,128]{2,1,0:T(8,128)(2,1)} %bitcast.106, f32[16,2560]{1,0:T(8,128)S(1)} %copy-done.10), kind=kLoop, calls=%fused_computation.8 | loop fusion | flops 15400960 | bytes 11960320 | tf_op jit(solution)/shard_map/reduce_sum | solution.py:203
  212.1 1.8 multiply_reduce_fusion.1
  (172 shorter events, 34.2 us)
Async XLA Ops:
  7.2 72.9 %all-gather.5.cloned.1.call-start = ((), (), s32[]{:S(2)}) async-start(), calls=%async_computation.1 | async-start | bytes 1183744 | tf_op jit(solution)/shard_map/all_gather | solution.py:105
  18.3 179.6 %all-gather.7.cloned.1.call-start = ((), (), s32[]{:S(2)}) async-start(), calls=%async_computation.2 | async-start | bytes 11141120 | tf_op jit(solution)/shard_map/all_gather | solution.py:82
  27.1 2.2 copy-start.16
  27.1 2.3 %copy-start.15 = (f32[2816]{0:T(1024)S(1)}, f32[2816]{0:T(1024)}, u32[]{:S(2)}) copy-start(f32[2816]{0:T(1024)} %param.17) | copy-start | bytes 33796
  29.3 8.7 %copy-start = (f32[256,2560]{1,0:T(8,128)}, f32[256,2560]{1,0:T(8,128)S(1)}, u32[]{:S(2)}) copy-start(f32[256,2560]{1,0:T(8,128)S(1)} %copy.178) | copy-start | bytes 7864324
  29.3 7.1 %copy-start.4 = (f32[256,2560]{1,0:T(8,128)S(1)}, f32[256,2560]{1,0:T(8,128)}, u32[]{:S(2)}) copy-start(f32[256,2560]{1,0:T(8,128)} %copy.183) | copy-start | bytes 7864324
  35.3 1.1 copy-start.3
  38.0 2.5 %copy-start.19 = (f32[40]{0:T(128)S(1)}, f32[40]{0:T(128)}, u32[]{:S(2)}) copy-start(f32[40]{0:T(128)} %param.20) | copy-start | bytes 484
  42.3 4.0 %copy-start.18 = (s32[16]{0:T(128)S(1)}, s32[16]{0:T(128)}, u32[]{:S(2)}) copy-start(s32[16]{0:T(128)} %param.15) | copy-start | bytes 196
  84.7 1.0 copy-start.7
  88.4 1.7 copy-start.1
  89.3 0.7 copy-start.8
  90.1 16.2 %copy-start.12 = (bf16[1,3,2816]{2,1,0:T(4,128)(2,1)}, bf16[1,3,2816]{2,1,0:T(4,128)(2,1)S(1)}, u32[]{:S(2)}) copy-start(bf16[1,3,2816]{2,1,0:T(4,128)(2,1)S(1)} %copy.220) | copy-start | bytes 50692
  94.1 4.9 %slice-start.3 = ((f32[16,17408]{1,0:T(8,128)}), f32[16,40]{1,0:T(8,128)S(1)}, s32[]{:S(2)}) async-start(f32[16,17408]{1,0:T(8,128)} %copy-done.7), calls=%async_computation.6 | async-start | bytes 16384 | tf_op jit(solution)/shard_map/slice | solution.py:119
  108.8 30.3 %all-to-all-start = ((bf16[3,16,160,128]{3,2,0,1:T(8,128)(2,1)}), bf16[3,16,160,128]{3,2,0,1:T(8,128)(2,1)}, u32[]{:S(2)}, u32[]{:S(2)}) async-start(bf16[3,16,160,128]{3,2,0,1:T(8,128)(2,1)} %copy.190), calls=%async_computation | async-start | bytes 3932160 | tf_op jit(solution)/shard_map/all_to_all | solution.py:189
  116.0 4.9 %copy-start.13 = (bf16[1,3,2816]{2,1,0:T(4,128)(2,1)S(1)}, bf16[1,3,2816]{2,1,0:T(4,128)(2,1)}, u32[]{:S(2)}) copy-start(bf16[1,3,2816]{2,1,0:T(4,128)(2,1)} %copy-done.12) | copy-start | bytes 50692
  116.3 4.8 %copy-start.14 = (pred[256,256]{1,0:T(8,128)(4,1)S(1)}, pred[256,256]{1,0:T(8,128)(4,1)}, u32[]{:S(2)}) copy-start(pred[256,256]{1,0:T(8,128)(4,1)} %fusion.26) | copy-start | bytes 196612
  125.9 3.2 %copy-start.9 = (bf16[16,3,2816]{2,0,1:T(8,128)(2,1)S(1)}, bf16[16,3,2816]{2,0,1:T(8,128)(2,1)}, u32[]{:S(2)}) copy-start(bf16[16,3,2816]{2,0,1:T(8,128)(2,1)} %copy-done.8) | copy-start | bytes 811012
  133.5 2.4 %copy-start.2 = (f32[4,2560,128]{2,1,0:T(8,128)}, f32[4,2560,128]{2,1,0:T(8,128)S(1)}, u32[]{:S(2)}) copy-start(f32[4,2560,128]{2,1,0:T(8,128)S(1)} %convolution_bitcast_fusion) | copy-start | bytes 15728644
  135.9 63.3 %copy-start.10 = (f32[16,2560]{1,0:T(8,128)S(1)}, f32[16,2560]{1,0:T(8,128)}, u32[]{:S(2)}) copy-start(f32[16,2560]{1,0:T(8,128)} %mul.335) | copy-start | bytes 491524
  197.9 14.0 %slice-start = ((s8[5242880]{0:T(1024)(128)(4,1)}), s8[4194304]{0:T(1024)(128)(4,1)S(1)}, s32[]{:S(2)}) async-start(s8[5242880]{0:T(1024)(128)(4,1)} %bitcast.103), calls=%async_computation.3 | async-start | bytes 8388608
  199.2 12.7 %slice-start.1 = ((s8[5242880]{0:T(1024)(128)(4,1)}), s8[1048576]{0:T(1024)(128)(4,1)S(1)}, s32[]{:S(2)}) async-start(s8[5242880]{0:T(1024)(128)(4,1)} %bitcast.103), calls=%async_computation.4 | async-start | bytes 2097152
  199.3 12.7 %copy-start.5 = (f32[256,2560]{1,0:T(8,128)S(1)}, f32[256,2560]{1,0:T(8,128)}, u32[]{:S(2)}) copy-start(f32[256,2560]{1,0:T(8,128)} %copy.187) | copy-start | bytes 7864324
  199.3 12.7 %copy-start.6 = (f32[256,2560]{1,0:T(8,128)S(1)}, f32[256,2560]{1,0:T(8,128)}, u32[]{:S(2)}) copy-start(f32[256,2560]{1,0:T(8,128)} %copy.188) | copy-start | bytes 7864324
  199.3 12.7 %copy-start.20 = (bf16[256,2560]{1,0:T(8,128)(2,1)S(1)}, bf16[256,2560]{1,0:T(8,128)(2,1)}, u32[]{:S(2)}) copy-start(bf16[256,2560]{1,0:T(8,128)(2,1)} %param.12) | copy-start | bytes 3932164
  212.0 1.9 copy-start.11
  212.0 2.7 %copy-start.17 = (f32[2560]{0:T(1024)S(1)}, f32[2560]{0:T(1024)}, u32[]{:S(2)}) copy-start(f32[2560]{0:T(1024)} %param.21) | copy-start | bytes 30724
  213.9 2.3 %slice-start.2 = ((f32[4,2560,128]{2,1,0:T(8,128)}), f32[3,2560,128]{2,1,0:T(8,128)S(1)}, s32[]{:S(2)}) async-start(f32[4,2560,128]{2,1,0:T(8,128)} %copy-done.2), calls=%async_computation.5 | async-start | bytes 7864320 | tf_op jit(solution)/shard_map/slice | solution.py:222
Sparse Core Ops, SparseCore 0:
  18.4 61.5 all-gather.4
  83.0 114.8 all-gather.6

commit v2 on v1

--- a/solution.py
+++ b/solution.py
@@ -22,7 +22,11 @@
 
 
 def per_head(x):
-    return jnp.repeat(x, HEAD_DIM, axis=-1)
+    expand = (
+        jnp.arange(HEADS * HEAD_DIM, dtype=jnp.int32)[None, :] // HEAD_DIM
+        == jnp.arange(HEADS, dtype=jnp.int32)[:, None]
+    ).astype(f32)
+    return jnp.matmul(x, expand, precision=lax.Precision.HIGHEST)
 
 
 def conv_rows(ext, ext_doc, out_doc, conv_weight, conv_bias):
@@ -102,7 +106,9 @@
     width = flat.shape[0]
     padded_width = -(-width // 128) * 128
     flat = jnp.pad(flat, (0, padded_width - width))
-    small = lax.all_gather(flat, "seq", axis=0, tiled=False)
+    small = lax.all_to_all(
+        jnp.broadcast_to(flat[None], (n, padded_width)), "seq", 0, 0, tiled=True
+    )
 
     slots = jnp.arange(n, dtype=jnp.int32)
     holder = jnp.sum(
@@ -198,15 +204,13 @@
             (1, 0, 2),
         ).astype(f32)
 
-    gs = gathered_states.astype(f32)
-    state_in = (
-        jnp.sum(
-            cross_dev[mine][:, :, None, None]
-            * gs.reshape(n, HEADS, HEAD_DIM, STATE),
-            axis=0,
-        ).reshape(INNER, STATE)
-        + lead_state[0]
-    )
+    own_cross = cross_dev[mine]
+    state_in = lead_state[0].reshape(HEADS, HEAD_DIM, STATE)
+    for k in range(n):
+        state_in = state_in + own_cross[k][:, None, None] * gathered_states[k].astype(
+            f32
+        ).reshape(HEADS, HEAD_DIM, STATE)
+    state_in = state_in.reshape(INNER, STATE)
     readout = jnp.dot(queries, state_in.astype(bf16).T, preferred_element_type=f32)
     carry_weight = jnp.exp(jnp.where((doc == prev_seq[mine])[:, None], lc, -jnp.inf))
     outputs = within + readout * per_head(carry_weight) + direct
@@ -216,7 +220,9 @@
 
     row_ids = me * rows_here + jnp.arange(rows_here, dtype=jnp.int32)
     row_head = row_ids // HEAD_DIM
-    gs_rows = lax.dynamic_slice_in_dim(gs, me * rows_here, rows_here, axis=1)
+    gs_rows = lax.dynamic_slice_in_dim(
+        gathered_states, me * rows_here, rows_here, axis=1
+    ).astype(f32)
     owner_cross = cross_dev[doc_owner][:, :, row_head]
     owner_in = jnp.einsum("dkr,krn->drn", owner_cross, gs_rows, precision=lax.Precision.HIGHEST)
     owner_in = owner_in + lax.dynamic_slice_in_dim(lead_state[1:], me * rows_here, rows_here, axis=1)

time: 225 us -> 201 us (0.89)
  matrix products: 14.7 us -> 37.5 us
  other arithmetic: 39.2 us -> 17.1 us
  local copies, waits for them, and re-layouts: 54.7 us -> 34.1 us
  waiting for transfers between devices: 92.7 us -> 81.6 us
  starting transfers between devices: 5.24 us -> 12.5 us
    all_gather x1 -> x0, waiting for transfers between devices: 32.4 us -> none  [body(): small = lax.all_gather(flat, 'seq', axis=0, tiled=False)]
    all_gather x1, waiting for transfers between devices: 57 us -> 71.3 us  [body(): lax.all_gather(state_part.astype(bf16), 'seq', axis=0, tiled=False)]
    dot_general x0 -> x8, matrix products: none -> 13.7 us  [per_head(): return jnp.matmul(x, expand, precision=lax.Precision.HIGHEST)]
    reduce_sum x1 -> x0, other arithmetic: 12.7 us -> none  [body(): jnp.sum(cross_dev[mine][:, :, None, None] * gs.reshape(n, HEADS, HEAD_DIM...]
    dot_general x1, matrix products: 1.84 us -> 11.5 us  [body(): jnp.dot(queries, state_in.astype(bf16).T, preferred_element_type=f32)]
    reshape x6 -> x1, local copies, waits for them, and re-layouts: 7.99 us -> 0.01 us  [the longest x5 7.99 us: per_head(): return jnp.repeat(x, HEAD_DIM, axis=-1)]
    all_to_all x0 -> x1, starting transfers between devices: none -> 7.75 us  [body(): lax.all_to_all(jnp.broadcast_to(flat[None], (n, padded_width)), 'seq', 0,...]
    all_to_all x0 -> x1, waiting for transfers between devices: none -> 6.32 us  [body(): lax.all_to_all(jnp.broadcast_to(flat[None], (n, padded_width)), 'seq', 0,...]
  transfers between devices with their start and end apart: 3 -> 3, of which waited for: 3 -> 3; matrix products, arithmetic and copies ran while one was open for 33% -> 21% of each run, Pallas kernels for 0% -> 0%
where the time goes in v2:
time: 201 us; the launch traced here: 200 us
  waiting for transfers between devices  81.6 us (41%)
  matrix products  37.5 us (19%)
  local copies, waits for them, and re-layouts  34.1 us (17%)
  between operations  17.3 us (9%)
  other arithmetic  17.1 us (9%)
  starting transfers between devices  12.5 us (6%)
    all_gather x1, waiting for transfers between devices, body(): lax.all_gather(state_part.astype(bf16), 'seq', axis=0, tiled=False)  71.3 us
    dot_general x8, matrix products, per_head(): return jnp.matmul(x, expand, precision=lax.Precision.HIGHEST)  13.7 us
    dot_general x1, matrix products, body(): jnp.dot(queries, state_in.astype(bf16).T, preferred_element_type=f32)  11.5 us
    all_to_all x1, starting transfers between devices, body(): lax.all_to_all(jnp.broadcast_to(flat[None], (n, padded_width)), 'seq', 0,...  7.75 us
    all_to_all x1, waiting for transfers between devices, body(): lax.all_to_all(jnp.broadcast_to(flat[None], (n, padded_width)), 'seq', 0,...  6.32 us
    unnamed x35, local copies, waits for them, and re-layouts  5.85 us
    all_to_all x1, starting transfers between devices, body(): lax.all_to_all(final_part.reshape(docs, n, rows_here, STATE), 'seq', 1, 1...  4.74 us
    dot_general x1, matrix products, body(): jnp.einsum('hts,shp->thp', mixing, scaled.reshape(STRETCH, HEADS, HEAD_DI...  4.4 us
  transfers between devices with their start and end apart: 3, of which 3 were waited for; matrix products, arithmetic and copies ran while one was open for 21% of the time, Pallas kernels for 0%

profile of v2, /device:TPU:1, one launch (start us, length us, event | category | flops | bytes accessed | tf_op | source)
XLA Modules:
  0.0 200.2 jit_solution(17449187387618398755)
XLA Ops:
  10.7 1.2 dynamic_slice.18
  17.0 1.6 broadcast_in_dim.148
  18.6 7.7 %all-to-all-start = ((f32[16,1,17408]{2,1,0:T(1,128)}), f32[16,1,17408]{2,1,0:T(1,128)}, u32[]{:S(2)}, u32[]{:S(2)}) async-start(f32[16,1,17408]{2,1,0:T(1,128)} %broadcast_in_dim.148), calls=%async_computation | async-start | bytes 2228224 | tf_op jit(solution)/shard_map/all_to_all | solution.py:109
  29.3 1.3 compare_and_fusion.1
  30.7 2.7 %multiply_convert_fusion.3 = bf16[256,2816]{1,0:T(8,128)(2,1)S(1)} fusion(bf16[256,2816]{1,0:T(8,128)(2,1)S(1)} %copy-done.7, f32[2816]{0:T(1024)S(1)} %get-tuple-element.4, f32[256]{0:T(256)S(1)} %get-tuple-element.42, f32[2816]{0:T(1024)S(1)} %get-tuple-element.5, f32[256]{0:T(256)S(1)} %get-tuple-element.43, f32[2816]{0:T(1024)S(1)} %get-tuple-element.3, ...), kind=kLoop, calls=%fused_computation.36 | loop fusion | flops 14417920 | bytes 2942976 | tf_op jit(solution)/shard_map/convert_element_type | solution.py:43
  34.6 6.3 %all-to-all-done = f32[16,1,17408]{2,1,0:T(1,128)} async-done(((f32[16,1,17408]{2,1,0:T(1,128)}), f32[16,1,17408]{2,1,0:T(1,128)}, u32[]{:S(2)}, u32[]{:S(2)}) %all-to-all-start) | async-done | bytes 1114144 | tf_op jit(solution)/shard_map/all_to_all | solution.py:109
  40.9 1.5 copy.174
  42.4 1.8 gather_fusion.1
  44.2 1.4 broadcast_select_fusion
  45.6 1.0 copy-done.6
  47.5 1.9 reshape.773
  50.4 3.6 %fusion.144 = (f32[256,2560]{1,0:T(8,128)}, bf16[256,2560]{1,0:T(8,128)(2,1)}, f32[256,2560]{1,0:T(8,128)S(1)}) fusion(bf16[253,2816]{1,0:T(8,128)(2,1)S(1)} %slice.362, bf16[3,2816]{1,0:T(4,128)(2,1)S(1)} %bitcast.178, s32[2560]{0:T(1024)S(1)} %add_select_fusion, bf16[256,40]{0,1:T(8,128)(2,1)S(1)} %copy-done.8, f32[40]{0:T(128)S(1)} %copy-done.12), kind=kOutput, calls=%fused_computation.298 | convolution fusion | flops 319344640 | bytes 8026272 | tf_op jit(solution)/shard_map/dot_general | solution.py:29
  54.0 1.4 fusion.9
  55.4 1.4 convolution_convert_fusion.1
  59.4 2.8 %fusion.74 = f32[256,2560]{1,0:T(8,128)} fusion(s32[2560]{0:T(1024)S(1)} %add_select_fusion, pred[256]{0:T(512)(128)(4,1)S(1)} %get-tuple-element.45, f32[40,2,128]{2,0,1:T(8,128)S(1)} %reduce-window.10, f32[40,2]{0,1:T(2,128)S(1)} %slice.251), kind=kOutput, calls=%fused_computation.129 | convolution fusion | flops 314695680 | bytes 2673216 | tf_op jit(solution)/shard_map/dot_general | solution.py:29
  62.2 4.0 %multiply_convert_fusion.1 = bf16[3,256,2560]{2,1,0:T(8,128)(2,1)S(1)} fusion(f32[256,2560]{1,0:T(8,128)S(1)} %copy-done.5, s32[2560]{0:T(1024)S(1)} %add_select_fusion, f32[256,40]{0,1:T(8,128)S(1)} %get-tuple-element.19, f32[3,40]{1,0:T(4,128)S(1)} %gather_fusion, pred[3,256]{1,0:T(4,128)(4,1)S(1)} %fusion.122), kind=kOutput, calls=%fused_computation.9 | convolution fusion | flops 947814400 | bytes 6606048 | tf_op jit(solution)/shard_map/dot_general | solution.py:29
  66.2 1.2 convolution_convert_fusion
  67.5 1.5 copy.139
  68.9 4.7 %all-to-all-start.1 = ((bf16[3,16,160,128]{3,2,0,1:T(8,128)(2,1)}), bf16[3,16,160,128]{3,2,0,1:T(8,128)(2,1)}, u32[]{:S(2)}, u32[]{:S(2)}) async-start(bf16[3,16,160,128]{3,2,0,1:T(8,128)(2,1)} %copy.139), calls=%async_computation.1 | async-start | bytes 3932160 | tf_op jit(solution)/shard_map/all_to_all | solution.py:195
  74.7 1.0 select_reduce_fusion
  77.6 4.3 %convolution_bitcast_fusion = f32[4,2560,128]{2,1,0:T(8,128)S(1)} fusion(f32[16,3,2560]{2,0,1:T(8,128)S(1)} %fusion.13, f32[4,16,2560]{2,1,0:T(8,128)S(1)} %fusion.80, bf16[16,3,2816]{2,0,1:T(8,128)(2,1)S(1)} %multiply_convert_fusion.6), kind=kOutput, calls=%fused_computation.16 | convolution fusion | flops 755466240 | bytes 6402048 | tf_op jit(solution)/shard_map/rxk,xn->rkn/dot_general | solution.py:163
  81.9 2.4 %copy-done.2 = f32[4,2560,128]{2,1,0:T(8,128)} copy-done((f32[4,2560,128]{2,1,0:T(8,128)}, f32[4,2560,128]{2,1,0:T(8,128)S(1)}, u32[]{:S(2)}) %copy-start.2) | copy-done | bytes 5242904
  87.5 1.6 copy.133
  89.2 4.4 %fusion = f32[40,64,256]{2,1,0:T(8,128)} fusion(bf16[256,40,64]{0,2,1:T(8,128)(2,1)S(1)} %bitcast.177, f32[40,256]{1,0:T(8,128)S(1)} %get-tuple-element.18, f32[256,256]{1,0:T(8,128)S(1)} %fusion.142, pred[256,256]{1,0:T(8,128)(4,1)S(1)} %fusion.84), kind=kOutput, calls=%fused_computation.10 | convolution fusion | flops 346030080 | bytes 4300800 | tf_op jit(solution)/shard_map/hts,shp->thp/dot_general | solution.py:175
  93.6 3.2 %copy.137 = f32[256,2560]{1,0:T(8,128)} copy(f32[256,2560]{0,1:T(8,128)} %bitcast.176) | data formatting | bytes 5242880 | tf_op jit(solution)/shard_map/reshape | solution.py:180
  99.3 3.9 %all-to-all-done.1 = bf16[3,16,160,128]{3,2,0,1:T(8,128)(2,1)} async-done(((bf16[3,16,160,128]{3,2,0,1:T(8,128)(2,1)}), bf16[3,16,160,128]{3,2,0,1:T(8,128)(2,1)}, u32[]{:S(2)}, u32[]{:S(2)}) %all-to-all-start.1) | async-done | bytes 1966112 | tf_op jit(solution)/shard_map/all_to_all | solution.py:195
  103.2 1.8 convert_reduce_fusion
  105.1 71.3 %all-gather.3.cloned.1.call-done = bf16[40960,128]{1,0:T(8,128)(2,1)} async-done(((bf16[2560,128]{1,0:T(8,128)(2,1)}), bf16[40960,128]{1,0:T(8,128)(2,1)}) %all-gather.3.cloned.1.call-update) | async-done | bytes 10485776 | tf_op jit(solution)/shard_map/all_gather | solution.py:86
  176.4 11.5 %multiply_reduce_fusion = (f32[256]{0:T(256)S(1)}, f32[256,2560]{1,0:T(8,128)S(1)}) fusion(bf16[256,2560]{1,0:T(8,128)(2,1)} %param.12, f32[2560]{0:T(1024)S(1)} %copy-done.14, bf16[253,2816]{1,0:T(8,128)(2,1)S(1)} %slice.362, bf16[3,2816]{1,0:T(4,128)(2,1)S(1)} %bitcast.181, f32[256,2560]{1,0:T(8,128)} %copy.137, f32[256,2560]{1,0:T(8,128)} %fusion.74, ...), kind=kOutput, calls=%fused_computation.42 | convolution fusion | flops 194445056 | bytes 24110080 | tf_op jit(solution)/shard_map/dot_general | solution.py:214
  187.9 1.1 constant_dynamic-slice_fusion
  189.9 1.3 multiply_convert_fusion.4
  191.2 1.2 slice-done
  (170 shorter events, 24.7 us)
Async XLA Ops:
  7.2 51.1 %copy-start = (f32[40]{0:T(128)S(1)}, f32[40]{0:T(128)}, u32[]{:S(2)}) copy-start(f32[40]{0:T(128)} %param.20) | copy-start | bytes 484
  17.0 9.4 %copy-start.13 = (s32[16]{0:T(128)S(1)}, s32[16]{0:T(128)}, u32[]{:S(2)}) copy-start(s32[16]{0:T(128)} %param.15) | copy-start | bytes 196
  17.0 10.9 %copy-start.10 = (f32[4,2816]{1,0:T(4,128)S(1)}, f32[4,2816]{1,0:T(4,128)}, u32[]{:S(2)}) copy-start(f32[4,2816]{1,0:T(4,128)} %param.16) | copy-start | bytes 135172
  18.6 12.1 %copy-start.7 = (bf16[256,2816]{1,0:T(8,128)(2,1)S(1)}, bf16[256,2816]{1,0:T(8,128)(2,1)}, u32[]{:S(2)}) copy-start(bf16[256,2816]{1,0:T(8,128)(2,1)} %param.11) | copy-start | bytes 4325380
  18.6 12.1 %copy-start.9 = (f32[2816]{0:T(1024)S(1)}, f32[2816]{0:T(1024)}, u32[]{:S(2)}) copy-start(f32[2816]{0:T(1024)} %param.17) | copy-start | bytes 33796
  18.6 22.3 %all-to-all-start = ((f32[16,1,17408]{2,1,0:T(1,128)}), f32[16,1,17408]{2,1,0:T(1,128)}, u32[]{:S(2)}, u32[]{:S(2)}) async-start(f32[16,1,17408]{2,1,0:T(1,128)} %broadcast_in_dim.148), calls=%async_computation | async-start | bytes 2228224 | tf_op jit(solution)/shard_map/all_to_all | solution.py:109
  26.3 150.1 %all-gather.3.cloned.1.call-start = ((), (), s32[]{:S(2)}) async-start(), calls=%async_computation.2 | async-start | bytes 11141120 | tf_op jit(solution)/shard_map/all_gather | solution.py:86
  33.3 1.1 copy-start.3
  45.6 1.0 copy-start.6
  49.7 0.7 copy-start.8
  49.7 0.7 copy-start.12
  50.4 3.6 %copy-start.4 = (bf16[256,2816]{1,0:T(8,128)(2,1)S(1)}, bf16[256,2816]{1,0:T(8,128)(2,1)}, u32[]{:S(2)}) copy-start(bf16[256,2816]{1,0:T(8,128)(2,1)} %copy-done.3) | copy-start | bytes 4325380
  59.4 2.8 %copy-start.5 = (f32[256,2560]{1,0:T(8,128)S(1)}, f32[256,2560]{1,0:T(8,128)}, u32[]{:S(2)}) copy-start(f32[256,2560]{1,0:T(8,128)} %get-tuple-element.10) | copy-start | bytes 7864324
  68.9 5.8 %slice-start.1 = ((f32[16,17408]{1,0:T(8,128)}), f32[16,40]{1,0:T(8,128)S(1)}, s32[]{:S(2)}) async-start(f32[16,17408]{1,0:T(8,128)} %copy-done.6), calls=%async_computation.4 | async-start | bytes 16384 | tf_op jit(solution)/shard_map/slice | solution.py:125
  68.9 34.3 %all-to-all-start.1 = ((bf16[3,16,160,128]{3,2,0,1:T(8,128)(2,1)}), bf16[3,16,160,128]{3,2,0,1:T(8,128)(2,1)}, u32[]{:S(2)}, u32[]{:S(2)}) async-start(bf16[3,16,160,128]{3,2,0,1:T(8,128)(2,1)} %copy.139), calls=%async_computation.1 | async-start | bytes 3932160 | tf_op jit(solution)/shard_map/all_to_all | solution.py:195
  81.8 2.4 %copy-start.2 = (f32[4,2560,128]{2,1,0:T(8,128)}, f32[4,2560,128]{2,1,0:T(8,128)S(1)}, u32[]{:S(2)}) copy-start(f32[4,2560,128]{2,1,0:T(8,128)S(1)} %convolution_bitcast_fusion) | copy-start | bytes 15728644
  97.6 78.8 %copy-start.14 = (f32[2560]{0:T(1024)S(1)}, f32[2560]{0:T(1024)}, u32[]{:S(2)}) copy-start(f32[2560]{0:T(1024)} %convolution_reduce_fusion) | copy-start | bytes 30724
  187.9 2.0 copy-start.11
  189.9 2.6 %slice-start = ((f32[4,2560,128]{2,1,0:T(8,128)}), f32[3,2560,128]{2,1,0:T(8,128)S(1)}, s32[]{:S(2)}) async-start(f32[4,2560,128]{2,1,0:T(8,128)} %copy-done.2), calls=%async_computation.3 | async-start | bytes 7864320 | tf_op jit(solution)/shard_map/slice | solution.py:228
  189.9 3.4 %copy-start.1 = (f32[40]{0:T(128)S(1)}, f32[40]{0:T(128)}, u32[]{:S(2)}) copy-start(f32[40]{0:T(128)} %param.20) | copy-start | bytes 484
Sparse Core Ops, SparseCore 0:
  56.9 119.4 all-gather.2

commit v3 on v2

--- a/solution.py
+++ b/solution.py
@@ -83,7 +83,6 @@
     )
     weighted_local = (scaled_local.astype(f32) * per_head(weight_end)).astype(bf16)
     state_part = jnp.dot(weighted_local.T, keys_local, preferred_element_type=f32)
-    gathered_states = lax.all_gather(state_part.astype(bf16), "seq", axis=0, tiled=False)
 
     doc_last = ends - 1
     doc_owner = doc_last // STRETCH
@@ -106,6 +105,8 @@
     width = flat.shape[0]
     padded_width = -(-width // 128) * 128
     flat = jnp.pad(flat, (0, padded_width - width))
+    flat, state_send = lax.optimization_barrier((flat, state_part.astype(bf16)))
+    gathered_states = lax.all_gather(state_send, "seq", axis=0, tiled=False)
     small = lax.all_to_all(
         jnp.broadcast_to(flat[None], (n, padded_width)), "seq", 0, 0, tiled=True
     )

time: 201 us -> 182 us (0.905)
  the two profiles are of different devices: /device:TPU:1 before, /device:TPU:482 now
where the time goes in v3:
time: 182 us; the launch traced here: 180 us
  local copies, waits for them, and re-layouts  73.6 us (40%)
  matrix products  37.2 us (20%)
  other arithmetic  29.1 us (16%)
  between operations  17.5 us (10%)
  starting transfers between devices  12.8 us (7%)
  waiting for transfers between devices  9.79 us (5%)
    mul x33, local copies, waits for them, and re-layouts, body(): own_cross[k][:, None, None]  22.8 us
    dot_general x8, matrix products, per_head(): return jnp.matmul(x, expand, precision=lax.Precision.HIGHEST)  12.5 us
    dot_general x1, matrix products, body(): jnp.dot(queries, state_in.astype(bf16).T, preferred_element_type=f32)  11.8 us
    all_to_all x1, waiting for transfers between devices, body(): lax.all_to_all(jnp.broadcast_to(flat[None], (n, padded_width)), 'seq', 0,...  9.76 us
    unnamed x101, local copies, waits for them, and re-layouts  7.73 us
    all_to_all x1, starting transfers between devices, body(): lax.all_to_all(jnp.broadcast_to(flat[None], (n, padded_width)), 'seq', 0,...  7.48 us
    all_to_all x1, starting transfers between devices, body(): lax.all_to_all(final_part.reshape(docs, n, rows_here, STATE), 'seq', 1, 1...  5.3 us
    gather x3, local copies, waits for them, and re-layouts, body(): owner_cross = cross_dev[doc_owner][:, :, row_head]  5.22 us
  transfers between devices with their start and end apart: 3, of which 1 were waited for; matrix products, arithmetic and copies ran while one was open for 54% of the time, Pallas kernels for 0%

profile of v3, /device:TPU:482, one launch (start us, length us, event | category | flops | bytes accessed | tf_op | source)
XLA Modules:
  0.0 180.1 jit_solution(1201841537292128523)
XLA Ops:
  24.7 2.7 %multiply_convert_fusion.3 = bf16[256,2816]{1,0:T(8,128)(2,1)S(1)} fusion(bf16[256,2816]{1,0:T(8,128)(2,1)S(1)} %copy-done.6, f32[2816]{0:T(1024)S(1)} %get-tuple-element.8, f32[256]{0:T(256)S(1)} %get-tuple-element.47, f32[2816]{0:T(1024)S(1)} %get-tuple-element.9, f32[256]{0:T(256)S(1)} %get-tuple-element.48, f32[2816]{0:T(1024)S(1)} %get-tuple-element.7, ...), kind=kLoop, calls=%fused_computation.36 | loop fusion | flops 14417920 | bytes 2942976 | tf_op jit(solution)/shard_map/convert_element_type | solution.py:43
  27.4 1.5 fusion.9
  29.0 1.4 convolution_convert_fusion.1
  30.4 1.6 broadcast_in_dim.149
  32.0 7.5 %all-to-all-start = ((f32[16,1,17408]{2,1,0:T(1,128)}), f32[16,1,17408]{2,1,0:T(1,128)}, u32[]{:S(2)}, u32[]{:S(2)}) async-start(f32[16,1,17408]{2,1,0:T(1,128)} %broadcast_in_dim.149), calls=%async_computation | async-start | bytes 2228224 | tf_op jit(solution)/shard_map/all_to_all | solution.py:110
  47.8 2.8 %fusion.74 = f32[256,2560]{1,0:T(8,128)} fusion(s32[2560]{0:T(1024)S(1)} %add_select_fusion, pred[256]{0:T(512)(128)(4,1)S(1)} %get-tuple-element.45, f32[40,2,128]{2,0,1:T(8,128)S(1)} %reduce-window.10, f32[40,2]{0,1:T(2,128)S(1)} %slice.251), kind=kOutput, calls=%fused_computation.129 | convolution fusion | flops 314695680 | bytes 2673216 | tf_op jit(solution)/shard_map/dot_general | solution.py:29
  50.6 9.8 %all-to-all-done = f32[16,1,17408]{2,1,0:T(1,128)} async-done(((f32[16,1,17408]{2,1,0:T(1,128)}), f32[16,1,17408]{2,1,0:T(1,128)}, u32[]{:S(2)}, u32[]{:S(2)}) %all-to-all-start) | async-done | bytes 1114144 | tf_op jit(solution)/shard_map/all_to_all | solution.py:110
  60.4 1.5 copy.174
  61.9 1.8 %gather_fusion.1 = f32[16,17408]{1,0:T(8,128)} fusion(f32[16,17408]{1,0:T(8,128)S(1)} %bitcast.173, s32[1024]{0:T(1024)S(1)} %pad_clamp_fusion.4), kind=kCustom, calls=%fused_computation.1 | custom fusion | bytes 2228288 | tf_op jit(solution)/shard_map/jit(_take)/gather | solution.py:118
  63.7 1.4 broadcast_select_fusion
  66.9 1.9 %reshape.773 = bf16[16,6,2816]{2,1,0:T(8,128)(2,1)S(1)} reshape(bf16[16,16896]{1,0:T(8,128)(2,1)} %slice.601) | data formatting | bytes 1081344 | tf_op jit(solution)/shard_map/convert.18
  70.9 1.7 select_reduce_fusion
  76.9 1.6 fusion.144
  78.5 3.9 %multiply_convert_fusion.1 = bf16[3,256,2560]{2,1,0:T(8,128)(2,1)S(1)} fusion(f32[256,2560]{1,0:T(8,128)S(1)} %get-tuple-element.14, s32[2560]{0:T(1024)S(1)} %add_select_fusion, f32[256,40]{0,1:T(8,128)S(1)} %get-tuple-element.23, f32[3,40]{1,0:T(4,128)S(1)} %copy-done.28, pred[3,256]{1,0:T(4,128)(4,1)S(1)} %copy-done.45), kind=kOutput, calls=%fused_computation.9 | convolution fusion | flops 947814400 | bytes 6606048 | tf_op jit(solution)/shard_map/dot_general | solution.py:29
  83.6 1.4 copy.139
  85.1 5.3 %all-to-all-start.1 = ((bf16[3,16,160,128]{3,2,0,1:T(8,128)(2,1)}), bf16[3,16,160,128]{3,2,0,1:T(8,128)(2,1)S(1)}, u32[]{:S(2)}, u32[]{:S(2)}) async-start(bf16[3,16,160,128]{3,2,0,1:T(8,128)(2,1)} %copy.139), calls=%async_computation.1 | async-start | bytes 3932160 | tf_op jit(solution)/shard_map/all_to_all | solution.py:196
  91.6 1.6 gather_fusion.3
  94.0 1.5 fusion.147
  95.5 1.5 select_bitcast_fusion
  97.0 1.4 fusion.153
  99.1 1.4 reshape.769
  100.5 1.4 reshape.768
  101.9 1.5 copy.141
  103.5 2.2 %gather_fusion.2 = f32[4,16,40]{2,1,0:T(8,128)} fusion(f32[16,16,40]{2,1,0:T(8,128)} %copy-done.11, s32[1024]{0:T(1024)} %pad_clamp_fusion.3), kind=kCustom, calls=%fused_computation.2 | custom fusion | bytes 20496 | tf_op jit(solution)/shard_map/gather | solution.py:160
  130.1 1.5 copy.144
  131.5 2.5 %gather_fusion.7 = f32[160,3,16]{2,1,0:T(4,128)} fusion(f32[3,16,40]{1,0,2:T(4,128)} %copy.144, s32[1024]{0:T(1024)S(1)} %copy-done.40), kind=kCustom, calls=%fused_computation.7 | custom fusion | bytes 62080 | tf_op jit(solution)/shard_map/gather | solution.py:227
  134.0 2.4 %copy.133 = bf16[256,2560]{0,1:T(8,128)(2,1)} copy(bf16[256,2560]{1,0:T(8,128)(2,1)} %get-tuple-element.15) | data formatting | bytes 2621440 | tf_op jit(solution)/shard_map/convert_element_type | solution.py:147
  137.8 4.3 %fusion = f32[40,64,256]{2,1,0:T(8,128)} fusion(bf16[256,40,64]{0,2,1:T(8,128)(2,1)S(1)} %bitcast.177, f32[40,256]{1,0:T(8,128)S(1)} %copy-done.26, f32[256,256]{1,0:T(8,128)S(1)} %fusion.142, pred[256,256]{1,0:T(8,128)(4,1)S(1)} %copy-done.23), kind=kOutput, calls=%fused_computation.10 | convolution fusion | flops 346030080 | bytes 4300800 | tf_op jit(solution)/shard_map/hts,shp->thp/dot_general | solution.py:176
  142.1 3.2 %copy.137 = f32[256,2560]{1,0:T(8,128)} copy(f32[256,2560]{0,1:T(8,128)} %bitcast.176) | data formatting | bytes 5242880 | tf_op jit(solution)/shard_map/reshape | solution.py:181
  147.4 5.0 %convolution_bitcast_fusion = f32[4,2560,128]{2,1,0:T(8,128)S(1)} fusion(f32[16,3,2560]{2,0,1:T(8,128)S(1)} %fusion.13, f32[4,16,2560]{2,1,0:T(8,128)S(1)} %fusion.80, bf16[16,3,2816]{2,0,1:T(8,128)(2,1)} %copy-done.9), kind=kOutput, calls=%fused_computation.16 | convolution fusion | flops 755466240 | bytes 6402048 | tf_op jit(solution)/shard_map/rxk,xn->rkn/dot_general | solution.py:164
  152.4 2.4 %copy-done.4 = f32[4,2560,128]{2,1,0:T(8,128)} copy-done((f32[4,2560,128]{2,1,0:T(8,128)}, f32[4,2560,128]{2,1,0:T(8,128)S(1)}, u32[]{:S(2)}) %copy-start.4) | copy-done | bytes 5242904
  155.9 11.8 %multiply_reduce_fusion = (f32[256]{0:T(256)S(1)}, f32[256,2560]{1,0:T(8,128)S(1)}) fusion(bf16[256,2560]{1,0:T(8,128)(2,1)} %param.12, f32[2560]{0:T(1024)} %convolution_reduce_fusion, bf16[253,2816]{1,0:T(8,128)(2,1)S(1)} %slice.364, bf16[3,2816]{1,0:T(4,128)(2,1)S(1)} %bitcast.181, f32[256,2560]{1,0:T(8,128)} %copy.137, f32[256,2560]{1,0:T(8,128)} %fusion.74, ...), kind=kOutput, calls=%fused_computation.42 | convolution fusion | flops 194445056 | bytes 24110080 | tf_op jit(solution)/shard_map/dot_general | solution.py:215
  (236 shorter events, 69.3 us)
Async XLA Ops:
  7.2 36.0 %copy-start = (f32[40]{0:T(128)S(1)}, f32[40]{0:T(128)}, u32[]{:S(2)}) copy-start(f32[40]{0:T(128)} %param.20) | copy-start | bytes 484
  7.2 16.2 %copy-start.46 = (f32[40]{0:T(128)S(1)}, f32[40]{0:T(128)}, u32[]{:S(2)}) copy-start(f32[40]{0:T(128)} %param.18) | copy-start | bytes 484
  7.2 16.2 %copy-start.22 = (bf16[256,40]{0,1:T(8,128)(2,1)S(1)}, bf16[256,40]{0,1:T(8,128)(2,1)}, u32[]{:S(2)}) copy-start(bf16[256,40]{0,1:T(8,128)(2,1)} %param.13) | copy-start | bytes 61444
  7.2 148.6 %all-gather.3.cloned.1.call-start = ((), (), s32[]{:S(2)}) async-start(), calls=%async_computation.2 | async-start | bytes 11141120 | tf_op jit(solution)/shard_map/all_gather | solution.py:109
  22.0 2.7 %copy-start.18 = (f32[2816]{0:T(1024)}, f32[2816]{0:T(1024)S(1)}, u32[]{:S(2)}) copy-start(f32[2816]{0:T(1024)S(1)} %get-tuple-element.9) | copy-start | bytes 33796
  24.7 2.7 %copy-start.2 = (f32[256,2560]{1,0:T(8,128)}, f32[256,2560]{1,0:T(8,128)S(1)}, u32[]{:S(2)}) copy-start(f32[256,2560]{1,0:T(8,128)S(1)} %fusion.76) | copy-start | bytes 7864324
  32.0 28.4 %all-to-all-start = ((f32[16,1,17408]{2,1,0:T(1,128)}), f32[16,1,17408]{2,1,0:T(1,128)}, u32[]{:S(2)}, u32[]{:S(2)}) async-start(f32[16,1,17408]{2,1,0:T(1,128)} %broadcast_in_dim.149), calls=%async_computation | async-start | bytes 2228224 | tf_op jit(solution)/shard_map/all_to_all | solution.py:110
  39.5 3.6 %copy-start.47 = (s32[16]{0:T(128)S(1)}, s32[16]{0:T(128)}, u32[]{:S(2)}) copy-start(s32[16]{0:T(128)} %param.15) | copy-start | bytes 196
  39.8 10.8 %copy-start.44 = (s32[1024]{0:T(1024)}, s32[1024]{0:T(1024)S(1)}, u32[]{:S(2)}) copy-start(s32[1024]{0:T(1024)S(1)} %pad_clamp_fusion.1) | copy-start | bytes 12292
  69.7 5.4 %copy-start.41 = (f32[16,3]{0,1:T(4,128)S(1)}, f32[16,3]{0,1:T(4,128)}, u32[]{:S(2)}) copy-start(f32[16,3]{0,1:T(4,128)} %get-tuple-element.42) | copy-start | bytes 580
  70.6 4.4 %copy-start.7 = (bf16[15,3,2816]{2,1,0:T(4,128)(2,1)S(1)}, bf16[15,3,2816]{2,1,0:T(4,128)(2,1)}, u32[]{:S(2)}) copy-start(bf16[15,3,2816]{2,1,0:T(4,128)(2,1)} %slice.360) | copy-start | bytes 760324
  70.6 4.6 %copy-start.19 = (f32[2816]{0:T(1024)S(1)}, f32[2816]{0:T(1024)}, u32[]{:S(2)}) copy-start(f32[2816]{0:T(1024)} %copy-done.18) | copy-start | bytes 33796
  70.6 4.6 %copy-start.25 = (f32[2816]{0:T(1024)S(1)}, f32[2816]{0:T(1024)}, u32[]{:S(2)}) copy-start(f32[2816]{0:T(1024)} %param.17) | copy-start | bytes 33796
  70.6 4.6 %copy-start.42 = (f32[16,3]{0,1:T(4,128)S(1)}, f32[16,3]{0,1:T(4,128)}, u32[]{:S(2)}) copy-start(f32[16,3]{0,1:T(4,128)} %get-tuple-element.43) | copy-start | bytes 580
  70.6 4.6 %copy-start.43 = (f32[16,3]{0,1:T(4,128)S(1)}, f32[16,3]{0,1:T(4,128)}, u32[]{:S(2)}) copy-start(f32[16,3]{0,1:T(4,128)} %get-tuple-element.44) | copy-start | bytes 580
  73.3 2.3 %copy-start.11 = (f32[16,16,40]{2,1,0:T(8,128)}, f32[16,16,40]{2,1,0:T(8,128)S(1)}, u32[]{:S(2)}) copy-start(f32[16,16,40]{2,1,0:T(8,128)S(1)} %exponential_select_fusion) | copy-start | bytes 122884
  75.0 1.8 %copy-start.3 = (f32[256,2560]{1,0:T(8,128)S(1)}, f32[256,2560]{1,0:T(8,128)}, u32[]{:S(2)}) copy-start(f32[256,2560]{1,0:T(8,128)} %copy-done.2) | copy-start | bytes 7864324
  75.7 2.8 %copy-start.15 = (bf16[1,3,2816]{2,1,0:T(4,128)(2,1)}, bf16[1,3,2816]{2,1,0:T(4,128)(2,1)S(1)}, u32[]{:S(2)}) copy-start(bf16[1,3,2816]{2,1,0:T(4,128)(2,1)S(1)} %copy.176) | copy-start | bytes 50692
  76.9 5.5 %copy-start.12 = (bf16[256,128]{1,0:T(8,128)(2,1)}, bf16[256,128]{1,0:T(8,128)(2,1)S(1)}, u32[]{:S(2)}) copy-start(bf16[256,128]{1,0:T(8,128)(2,1)S(1)} %pad_maximum_fusion.1) | copy-start | bytes 196612
  85.1 5.3 %copy-start.40 = (s32[1024]{0:T(1024)S(1)}, s32[1024]{0:T(1024)}, u32[]{:S(2)}) copy-start(s32[1024]{0:T(1024)} %pad_clamp_fusion) | copy-start | bytes 12292
  85.1 69.8 %all-to-all-start.1 = ((bf16[3,16,160,128]{3,2,0,1:T(8,128)(2,1)}), bf16[3,16,160,128]{3,2,0,1:T(8,128)(2,1)S(1)}, u32[]{:S(2)}, u32[]{:S(2)}) async-start(bf16[3,16,160,128]{3,2,0,1:T(8,128)(2,1)} %copy.139), calls=%async_computation.1 | async-start | bytes 3932160 | tf_op jit(solution)/shard_map/all_to_all | solution.py:196
  128.7 7.8 %copy-start.13 = (bf16[256,128]{1,0:T(8,128)(2,1)S(1)}, bf16[256,128]{1,0:T(8,128)(2,1)}, u32[]{:S(2)}) copy-start(bf16[256,128]{1,0:T(8,128)(2,1)} %copy-done.12) | copy-start | bytes 196612
  128.7 7.8 %copy-start.16 = (bf16[1,3,2816]{2,1,0:T(4,128)(2,1)S(1)}, bf16[1,3,2816]{2,1,0:T(4,128)(2,1)}, u32[]{:S(2)}) copy-start(bf16[1,3,2816]{2,1,0:T(4,128)(2,1)} %copy-done.15) | copy-start | bytes 50692
  142.1 3.2 %copy-start.17 = (f32[4,16,40]{2,1,0:T(8,128)S(1)}, f32[4,16,40]{2,1,0:T(8,128)}, u32[]{:S(2)}) copy-start(f32[4,16,40]{2,1,0:T(8,128)} %gather_fusion.2) | copy-start | bytes 30724
  142.1 3.7 %copy-start.20 = (f32[16,3,40]{2,1,0:T(4,128)S(1)}, f32[16,3,40]{2,1,0:T(4,128)}, u32[]{:S(2)}) copy-start(f32[16,3,40]{2,1,0:T(4,128)} %reshape.768) | copy-start | bytes 23044
  145.3 1.7 copy-start.21
  152.4 2.4 %copy-start.4 = (f32[4,2560,128]{2,1,0:T(8,128)}, f32[4,2560,128]{2,1,0:T(8,128)S(1)}, u32[]{:S(2)}) copy-start(f32[4,2560,128]{2,1,0:T(8,128)S(1)} %convolution_bitcast_fusion) | copy-start | bytes 15728644
  167.7 2.0 %copy-start.30 = (f32[2560]{0:T(1024)S(1)}, f32[2560]{0:T(1024)}, u32[]{:S(2)}) copy-start(f32[2560]{0:T(1024)} %param.21) | copy-start | bytes 30724
  168.9 2.2 %copy-start.10 = (f32[3,160,128]{2,1,0:T(8,128)S(1)}, f32[3,160,128]{2,1,0:T(8,128)}, u32[]{:S(2)}) copy-start(f32[3,160,128]{2,1,0:T(8,128)} %convert_reduce_fusion) | copy-start | bytes 737284
  169.8 2.6 %slice-start = ((f32[4,2560,128]{2,1,0:T(8,128)}), f32[3,2560,128]{2,1,0:T(8,128)S(1)}, s32[]{:S(2)}) async-start(f32[4,2560,128]{2,1,0:T(8,128)} %copy-done.4), calls=%async_computation.3 | async-start | bytes 7864320 | tf_op jit(solution)/shard_map/slice | solution.py:229
  169.8 2.6 %copy-start.29 = (f32[3,160]{1,0:T(4,128)S(1)}, f32[3,160]{1,0:T(4,128)}, u32[]{:S(2)}) copy-start(f32[3,160]{1,0:T(4,128)} %copy.141) | copy-start | bytes 5764
  169.8 3.4 %copy-start.1 = (f32[40]{0:T(128)S(1)}, f32[40]{0:T(128)}, u32[]{:S(2)}) copy-start(f32[40]{0:T(128)} %param.20) | copy-start | bytes 484
  (20 other events, 24.0 us)
Sparse Core Ops, SparseCore 0:
  30.5 115.9 all-gather.2

commit v4 on v2

--- a/solution.py
+++ b/solution.py
@@ -12,6 +12,7 @@
 CHANNELS = 2816
 LEAD = KERNEL - 1
 FINAL_VIA_ALL_TO_ALL = True
+HEADS_ON_GATHER = 25
 
 f32 = jnp.float32
 bf16 = jnp.bfloat16
@@ -83,7 +84,6 @@
     )
     weighted_local = (scaled_local.astype(f32) * per_head(weight_end)).astype(bf16)
     state_part = jnp.dot(weighted_local.T, keys_local, preferred_element_type=f32)
-    gathered_states = lax.all_gather(state_part.astype(bf16), "seq", axis=0, tiled=False)
 
     doc_last = ends - 1
     doc_owner = doc_last // STRETCH
@@ -106,6 +106,13 @@
     width = flat.shape[0]
     padded_width = -(-width // 128) * 128
     flat = jnp.pad(flat, (0, padded_width - width))
+    split = HEADS_ON_GATHER * HEAD_DIM
+    state_bf = state_part.astype(bf16)
+    flat, send_a, send_b = lax.optimization_barrier((flat, state_bf[:split], state_bf[split:]))
+    gathered_a = lax.all_gather(send_a, "seq", axis=0, tiled=False)
+    gathered_b = lax.all_to_all(
+        jnp.broadcast_to(send_b[None], (n,) + send_b.shape), "seq", 0, 0, tiled=True
+    )
     small = lax.all_to_all(
         jnp.broadcast_to(flat[None], (n, padded_width)), "seq", 0, 0, tiled=True
     )
@@ -191,6 +198,7 @@
     final_part = jnp.einsum(
         "dsk,sn->dkn", final_weighted, keys, preferred_element_type=f32
     ).astype(bf16)
+    final_part, gathered_b = lax.optimization_barrier((final_part, gathered_b))
     if FINAL_VIA_ALL_TO_ALL:
         parts_in = lax.all_to_all(
             final_part.reshape(docs, n, rows_here, STATE), "seq", 1, 1, tiled=True
@@ -204,13 +212,13 @@
             (1, 0, 2),
         ).astype(f32)
 
-    own_cross = cross_dev[mine]
-    state_in = lead_state[0].reshape(HEADS, HEAD_DIM, STATE)
+    own_w = per_head(cross_dev[mine])
+    state_a = lead_state[0][:split]
+    state_b = lead_state[0][split:]
     for k in range(n):
-        state_in = state_in + own_cross[k][:, None, None] * gathered_states[k].astype(
-            f32
-        ).reshape(HEADS, HEAD_DIM, STATE)
-    state_in = state_in.reshape(INNER, STATE)
+        state_a = state_a + own_w[k, :split][:, None] * gathered_a[k].astype(f32)
+        state_b = state_b + own_w[k, split:][:, None] * gathered_b[k].astype(f32)
+    state_in = jnp.concatenate([state_a, state_b], 0)
     readout = jnp.dot(queries, state_in.astype(bf16).T, preferred_element_type=f32)
     carry_weight = jnp.exp(jnp.where((doc == prev_seq[mine])[:, None], lc, -jnp.inf))
     outputs = within + readout * per_head(carry_weight) + direct
@@ -220,9 +228,14 @@
 
     row_ids = me * rows_here + jnp.arange(rows_here, dtype=jnp.int32)
     row_head = row_ids // HEAD_DIM
-    gs_rows = lax.dynamic_slice_in_dim(
-        gathered_states, me * rows_here, rows_here, axis=1
-    ).astype(f32)
+    first_row = me * rows_here
+    rows_a = lax.dynamic_slice_in_dim(
+        gathered_a, jnp.clip(first_row, 0, split - rows_here), rows_here, axis=1
+    )
+    rows_b = lax.dynamic_slice_in_dim(
+        gathered_b, jnp.clip(first_row - split, 0, INNER - split - rows_here), rows_here, axis=1
+    )
+    gs_rows = jnp.where(first_row < split, rows_a, rows_b).astype(f32)
     owner_cross = cross_dev[doc_owner][:, :, row_head]
     owner_in = jnp.einsum("dkr,krn->drn", owner_cross, gs_rows, precision=lax.Precision.HIGHEST)
     owner_in = owner_in + lax.dynamic_slice_in_dim(lead_state[1:], me * rows_here, rows_here, axis=1)

time: 201 us -> 217 us (1.080)
  the two profiles are of different devices: /device:TPU:1 before, /device:TPU:128 now
where the time goes in v4:
time: 217 us; the launch traced here: 215 us
  waiting for transfers between devices  62.8 us (29%)
  other arithmetic  48.2 us (22%)
  local copies, waits for them, and re-layouts  41.7 us (19%)
  matrix products  28.9 us (13%)
  between operations  17.8 us (8%)
  starting transfers between devices  15.9 us (7%)
    all_to_all x1, waiting for transfers between devices, body(): lax.all_to_all(jnp.broadcast_to(send_b[None], (n,) + send_b.shape), 'seq'...  33.4 us
    another operation x6, other arithmetic  17.1 us
    all_to_all x1, waiting for transfers between devices, body(): lax.all_to_all(final_part.reshape(docs, n, rows_here, STATE), 'seq', 1, 1...  16.5 us
    dot_general x9, matrix products, per_head(): return jnp.matmul(x, expand, precision=lax.Precision.HIGHEST)  12.6 us
    all_to_all x1, waiting for transfers between devices, body(): lax.all_to_all(jnp.broadcast_to(flat[None], (n, padded_width)), 'seq', 0,...  8.2 us
    all_to_all x1, starting transfers between devices, body(): lax.all_to_all(jnp.broadcast_to(flat[None], (n, padded_width)), 'seq', 0,...  7.07 us
    convert_element_type x2, other arithmetic, conv_rows(): return jax.nn.silu(accum).astype(bf16)  6.32 us
    gather x3, local copies, waits for them, and re-layouts, body(): owner_cross = cross_dev[doc_owner][:, :, row_head]  6.24 us
  transfers between devices with their start and end apart: 4, of which 4 were waited for; matrix products, arithmetic and copies ran while one was open for 33% of the time, Pallas kernels for 0%

profile of v4, /device:TPU:128, one launch (start us, length us, event | category | flops | bytes accessed | tf_op | source)
XLA Modules:
  0.0 215.2 jit_solution(6184824891452270122)
XLA Ops:
  18.8 2.0 fusion.64
  22.3 1.8 broadcast_compare_fusion
  24.0 5.9 %multiply_convert_fusion.3 = bf16[256,2816]{1,0:T(8,128)(2,1)S(1)} fusion(bf16[256,2816]{1,0:T(8,128)(2,1)} %param.11, f32[2816]{0:T(1024)S(1)} %get-tuple-element.30, f32[256]{0:T(256)S(1)} %get-tuple-element.69, f32[2816]{0:T(1024)S(1)} %get-tuple-element.31, f32[256]{0:T(256)S(1)} %get-tuple-element.70, f32[2816]{0:T(1024)S(1)} %get-tuple-element.29, ...), kind=kLoop, calls=%fused_computation.36 | loop fusion | flops 14417920 | bytes 2942976 | tf_op jit(solution)/shard_map/convert_element_type | solution.py:44
  30.1 1.5 fusion.9
  39.6 1.6 broadcast_in_dim.151
  41.2 7.1 %all-to-all-start = ((f32[16,1,17408]{2,1,0:T(1,128)}), f32[16,1,17408]{2,1,0:T(1,128)}, u32[]{:S(2)}, u32[]{:S(2)}) async-start(f32[16,1,17408]{2,1,0:T(1,128)} %broadcast_in_dim.151), calls=%async_computation | async-start | bytes 2228224 | tf_op jit(solution)/shard_map/all_to_all | solution.py:116
  55.7 2.9 %fusion.62 = f32[256,2560]{1,0:T(8,128)} fusion(s32[2560]{0:T(1024)S(1)} %add_select_fusion, pred[256]{0:T(512)(128)(4,1)S(1)} %copy-done.48, f32[40,2,128]{2,0,1:T(8,128)S(1)} %copy-done.12, f32[40,2]{0,1:T(2,128)S(1)} %copy-done.37), kind=kOutput, calls=%fused_computation.136 | convolution fusion | flops 314695680 | bytes 2673216 | tf_op jit(solution)/shard_map/dot_general | solution.py:30
  58.6 8.2 %all-to-all-done = f32[16,1,17408]{2,1,0:T(1,128)} async-done(((f32[16,1,17408]{2,1,0:T(1,128)}), f32[16,1,17408]{2,1,0:T(1,128)}, u32[]{:S(2)}, u32[]{:S(2)}) %all-to-all-start) | async-done | bytes 1114144 | tf_op jit(solution)/shard_map/all_to_all | solution.py:116
  66.8 2.7 %broadcast_in_dim.171 = bf16[16,960,128]{2,1,0:T(8,128)(2,1)} broadcast(bf16[960,128]{1,0:T(8,128)(2,1)S(1)} %slice-done.1), dimensions={1,2} | broadcast | bytes 4177920 | tf_op jit(solution)/shard_map/broadcast_in_dim | solution.py:114
  69.5 4.7 %all-to-all-start.1 = ((bf16[16,960,128]{2,1,0:T(8,128)(2,1)}), bf16[16,960,128]{2,1,0:T(8,128)(2,1)}, u32[]{:S(2)}, u32[]{:S(2)}) async-start(bf16[16,960,128]{2,1,0:T(8,128)(2,1)} %broadcast_in_dim.171), calls=%async_computation.1 | async-start | bytes 7864320 | tf_op jit(solution)/shard_map/all_to_all | solution.py:113
  74.2 1.5 copy.173
  75.7 1.8 gather_fusion.1
  80.8 1.9 reshape.726
  90.9 6.0 %convolution_bitcast_fusion = f32[4,2560,128]{2,1,0:T(8,128)} fusion(f32[16,3,2560]{2,0,1:T(8,128)S(1)} %fusion.13, f32[4,16,2560]{2,1,0:T(8,128)S(1)} %fusion.68, bf16[16,3,2816]{2,0,1:T(8,128)(2,1)S(1)} %multiply_convert_fusion.6), kind=kOutput, calls=%fused_computation.16 | convolution fusion | flops 755466240 | bytes 6402048 | tf_op jit(solution)/shard_map/rxk,xn->rkn/dot_general | solution.py:170
  96.9 1.6 fusion.134
  98.5 3.9 %multiply_convert_fusion.1 = bf16[3,256,2560]{2,1,0:T(8,128)(2,1)S(1)} fusion(f32[256,2560]{1,0:T(8,128)S(1)} %get-tuple-element.36, s32[2560]{0:T(1024)S(1)} %add_select_fusion, f32[256,40]{0,1:T(8,128)S(1)} %copy-done.15, f32[3,40]{1,0:T(4,128)S(1)} %copy-done.34, pred[3,256]{1,0:T(4,128)(4,1)S(1)} %copy-done.43), kind=kOutput, calls=%fused_computation.9 | convolution fusion | flops 947814400 | bytes 6606048 | tf_op jit(solution)/shard_map/dot_general | solution.py:30
  103.7 33.4 %all-to-all-done.1 = bf16[16,960,128]{2,1,0:T(8,128)(2,1)} async-done(((bf16[16,960,128]{2,1,0:T(8,128)(2,1)}), bf16[16,960,128]{2,1,0:T(8,128)(2,1)}, u32[]{:S(2)}, u32[]{:S(2)}) %all-to-all-start.1) | async-done | bytes 3932192 | tf_op jit(solution)/shard_map/all_to_all | solution.py:113
  138.4 4.1 %all-to-all-start.2 = ((bf16[3,16,160,128]{3,2,0,1:T(8,128)(2,1)}), bf16[3,16,160,128]{3,2,0,1:T(8,128)(2,1)S(1)}, u32[]{:S(2)}, u32[]{:S(2)}) async-start(bf16[3,16,160,128]{3,2,0,1:T(8,128)(2,1)} %copy.139), calls=%async_computation.2 | async-start | bytes 3932160 | tf_op jit(solution)/shard_map/all_to_all | solution.py:203
  142.5 1.5 select_bitcast_fusion
  144.0 1.6 copy.142
  145.7 2.2 %gather_fusion.6 = f32[3,16,40]{2,1,0:T(8,128)} fusion(f32[16,16,40]{2,1,0:T(8,128)} %copy.142, s32[1024]{0:T(1024)} %copy-done.42), kind=kCustom, calls=%fused_computation.6 | custom fusion | bytes 15372 | tf_op jit(solution)/shard_map/gather | solution.py:239
  149.3 2.6 %gather_fusion.7 = f32[160,3,16]{2,1,0:T(4,128)} fusion(f32[3,16,40]{1,0,2:T(4,128)} %copy.143, s32[1024]{0:T(1024)} %pad_clamp_fusion), kind=kCustom, calls=%fused_computation.7 | custom fusion | bytes 62080 | tf_op jit(solution)/shard_map/gather | solution.py:239
  151.9 1.6 copy.141
  153.5 2.4 %copy.133 = bf16[256,2560]{0,1:T(8,128)(2,1)} copy(bf16[256,2560]{1,0:T(8,128)(2,1)} %get-tuple-element.37) | data formatting | bytes 2621440 | tf_op jit(solution)/shard_map/convert_element_type | solution.py:153
  155.9 5.0 %fusion = f32[40,64,256]{2,1,0:T(8,128)} fusion(bf16[256,40,64]{0,2,1:T(8,128)(2,1)} %bitcast.244, f32[40,256]{1,0:T(8,128)} %get-tuple-element.60, f32[256,256]{1,0:T(8,128)} %fusion.132, pred[256,256]{1,0:T(8,128)(4,1)} %fusion.72), kind=kOutput, calls=%fused_computation.10 | convolution fusion | flops 346030080 | bytes 4300800 | tf_op jit(solution)/shard_map/hts,shp->thp/dot_general | solution.py:182
  160.8 3.3 %copy.138 = f32[256,2560]{1,0:T(8,128)} copy(f32[256,2560]{0,1:T(8,128)} %bitcast.243) | data formatting | bytes 5242880 | tf_op jit(solution)/shard_map/reshape | solution.py:187
  165.0 5.8 %fusion.60 = bf16[960,128]{1,0:T(8,128)(2,1)} fusion(f32[4,2560,128]{2,1,0:T(8,128)} %convolution_bitcast_fusion, bf16[16,960,128]{2,1,0:T(8,128)(2,1)} %all-to-all-done.1, f32[960]{0:T(1024)S(1)} %bitcast.252, f32[960]{0:T(1024)S(1)} %bitcast.253, f32[960]{0:T(1024)S(1)} %bitcast.254, f32[960]{0:T(1024)S(1)} %bitcast.255, f32[960]{0:T(1024)S(1)} %bitcast.256, ...), kind=kLoop, calls=%fused_computation.133 | loop fusion | flops 6021120 | bytes 4730880 | tf_op jit(solution)/shard_map/convert.34
  170.8 16.5 %all-to-all-done.2 = bf16[3,16,160,128]{3,2,0,1:T(8,128)(2,1)S(1)} async-done(((bf16[3,16,160,128]{3,2,0,1:T(8,128)(2,1)}), bf16[3,16,160,128]{3,2,0,1:T(8,128)(2,1)S(1)}, u32[]{:S(2)}, u32[]{:S(2)}) %all-to-all-start.2) | async-done | bytes 1966112 | tf_op jit(solution)/shard_map/all_to_all | solution.py:203
  188.3 4.0 %all-gather.3.cloned.1.call-done = bf16[25600,128]{1,0:T(8,128)(2,1)} async-done(((bf16[1600,128]{1,0:T(8,128)(2,1)}), bf16[25600,128]{1,0:T(8,128)(2,1)}) %all-gather.3.cloned.1.call-update) | async-done | bytes 6553616 | tf_op jit(solution)/shard_map/all_gather | solution.py:112
  192.3 9.1 %fusion.38 = bf16[1600,128]{1,0:T(8,128)(2,1)S(1)} fusion(f32[4,2560,128]{2,1,0:T(8,128)} %convolution_bitcast_fusion, bf16[25600,128]{1,0:T(8,128)(2,1)} %all-gather.3.cloned.1.call-done, f32[1600]{0:T(1024)S(1)} %get-tuple-element.13, f32[1600]{0:T(1024)S(1)} %get-tuple-element.14, f32[1600]{0:T(1024)S(1)} %get-tuple-element.15, ...), kind=kLoop, calls=%fused_computation.89 | loop fusion | flops 10035200 | bytes 7884800 | tf_op jit(solution)/shard_map/convert.33
  201.5 1.8 multiply_reduce_fusion
  203.3 1.8 dynamic-slice_select_fusion
  (225 shorter events, 45.7 us)
Async XLA Ops:
  7.2 46.9 %copy-start = (f32[40]{0:T(128)S(1)}, f32[40]{0:T(128)}, u32[]{:S(2)}) copy-start(f32[40]{0:T(128)} %param.20) | copy-start | bytes 484
  7.2 16.9 %copy-start.28 = (f32[2816]{0:T(1024)S(1)}, f32[2816]{0:T(1024)}, u32[]{:S(2)}) copy-start(f32[2816]{0:T(1024)} %param.17) | copy-start | bytes 33796
  10.8 23.0 %copy-start.40 = (s32[3,1]{0,1:T(1,128)}, s32[3,1]{0,1:T(1,128)S(1)}, u32[]{:S(2)}) copy-start(s32[3,1]{0,1:T(1,128)S(1)} %reduce-window.14) | copy-start | bytes 40
  13.4 19.7 %copy-start.30 = (s32[256]{0:T(256)}, s32[256]{0:T(256)S(1)}, u32[]{:S(2)}) copy-start(s32[256]{0:T(256)S(1)} %convert_reduce_fusion.2) | copy-start | bytes 3076
  15.0 15.0 %copy-start.20 = (f32[2816]{0:T(1024)}, f32[2816]{0:T(1024)S(1)}, u32[]{:S(2)}) copy-start(f32[2816]{0:T(1024)S(1)} %get-tuple-element.28) | copy-start | bytes 33796
  15.0 15.0 %copy-start.22 = (f32[2816]{0:T(1024)}, f32[2816]{0:T(1024)S(1)}, u32[]{:S(2)}) copy-start(f32[2816]{0:T(1024)S(1)} %get-tuple-element.29) | copy-start | bytes 33796
  15.0 15.0 %copy-start.24 = (f32[2816]{0:T(1024)}, f32[2816]{0:T(1024)S(1)}, u32[]{:S(2)}) copy-start(f32[2816]{0:T(1024)S(1)} %get-tuple-element.30) | copy-start | bytes 33796
  15.0 15.0 %copy-start.26 = (f32[2816]{0:T(1024)}, f32[2816]{0:T(1024)S(1)}, u32[]{:S(2)}) copy-start(f32[2816]{0:T(1024)S(1)} %get-tuple-element.31) | copy-start | bytes 33796
  17.7 12.3 %copy-start.11 = (f32[40,2,128]{2,0,1:T(8,128)}, f32[40,2,128]{2,0,1:T(8,128)S(1)}, u32[]{:S(2)}) copy-start(f32[40,2,128]{2,0,1:T(8,128)S(1)} %reduce-window.10) | copy-start | bytes 122884
  18.0 12.1 %copy-start.36 = (f32[40,2]{0,1:T(2,128)}, f32[40,2]{0,1:T(2,128)S(1)}, u32[]{:S(2)}) copy-start(f32[40,2]{0,1:T(2,128)S(1)} %slice.350) | copy-start | bytes 964
  18.7 15.0 %copy-start.14 = (f32[256,40]{0,1:T(8,128)}, f32[256,40]{0,1:T(8,128)S(1)}, u32[]{:S(2)}) copy-start(f32[256,40]{0,1:T(8,128)S(1)} %get-tuple-element.61) | copy-start | bytes 122884
  18.8 11.2 %copy-start.39 = (f32[40]{0:T(128)}, f32[40]{0:T(128)S(1)}, u32[]{:S(2)}) copy-start(f32[40]{0:T(128)S(1)} %slice_reduce_fusion.1) | copy-start | bytes 484
  20.9 10.7 %copy-start.2 = (f32[256,2560]{1,0:T(8,128)}, f32[256,2560]{1,0:T(8,128)S(1)}, u32[]{:S(2)}) copy-start(f32[256,2560]{1,0:T(8,128)S(1)} %fusion.64) | copy-start | bytes 7864324
  32.2 9.0 %copy-start.8 = (bf16[2560,128]{1,0:T(8,128)(2,1)}, bf16[2560,128]{1,0:T(8,128)(2,1)S(1)}, u32[]{:S(2)}) copy-start(bf16[2560,128]{1,0:T(8,128)(2,1)S(1)} %convolution_convert_fusion.1) | copy-start | bytes 1966084
  33.1 16.0 %copy-start.50 = (s32[16]{0:T(128)S(1)}, s32[16]{0:T(128)}, u32[]{:S(2)}) copy-start(s32[16]{0:T(128)} %param.15) | copy-start | bytes 196
  33.1 17.4 %copy-start.46 = (s32[16]{0:T(128)S(1)}, s32[16]{0:T(128)}, u32[]{:S(2)}) copy-start(s32[16]{0:T(128)} %get-tuple-element.32) | copy-start | bytes 196
  33.1 17.5 %copy-start.47 = (s32[16]{0:T(128)S(1)}, s32[16]{0:T(128)}, u32[]{:S(2)}) copy-start(s32[16]{0:T(128)} %get-tuple-element.74) | copy-start | bytes 196
  33.6 15.5 %copy-start.31 = (s32[256]{0:T(256)S(1)}, s32[256]{0:T(256)}, u32[]{:S(2)}) copy-start(s32[256]{0:T(256)} %copy-done.30) | copy-start | bytes 3076
  34.5 15.9 %copy-start.41 = (s32[3,1]{0,1:T(1,128)S(1)}, s32[3,1]{0,1:T(1,128)}, u32[]{:S(2)}) copy-start(s32[3,1]{0,1:T(1,128)} %copy-done.40) | copy-start | bytes 40
  35.3 18.4 %copy-start.5 = (bf16[256,2816]{1,0:T(8,128)(2,1)S(1)}, bf16[256,2816]{1,0:T(8,128)(2,1)}, u32[]{:S(2)}) copy-start(bf16[256,2816]{1,0:T(8,128)(2,1)} %copy-done.4) | copy-start | bytes 4325380
  41.2 25.6 %all-to-all-start = ((f32[16,1,17408]{2,1,0:T(1,128)}), f32[16,1,17408]{2,1,0:T(1,128)}, u32[]{:S(2)}, u32[]{:S(2)}) async-start(f32[16,1,17408]{2,1,0:T(1,128)} %broadcast_in_dim.151), calls=%async_computation | async-start | bytes 2228224 | tf_op jit(solution)/shard_map/all_to_all | solution.py:116
  48.3 144.0 %all-gather.3.cloned.1.call-start = ((), (), s32[]{:S(2)}) async-start(), calls=%async_computation.3 | async-start | bytes 6963200 | tf_op jit(solution)/shard_map/all_gather | solution.py:112
  53.7 13.1 %slice-start.1 = ((bf16[2560,128]{1,0:T(8,128)(2,1)}), bf16[960,128]{1,0:T(8,128)(2,1)S(1)}, s32[]{:S(2)}) async-start(bf16[2560,128]{1,0:T(8,128)(2,1)} %copy-done.8), calls=%async_computation.5 | async-start | bytes 491520 | tf_op jit(solution)/shard_map/slice | solution.py:111
  69.5 67.6 %all-to-all-start.1 = ((bf16[16,960,128]{2,1,0:T(8,128)(2,1)}), bf16[16,960,128]{2,1,0:T(8,128)(2,1)}, u32[]{:S(2)}, u32[]{:S(2)}) async-start(bf16[16,960,128]{2,1,0:T(8,128)(2,1)} %broadcast_in_dim.171), calls=%async_computation.1 | async-start | bytes 7864320 | tf_op jit(solution)/shard_map/all_to_all | solution.py:113
  83.7 13.2 %copy-start.17 = (bf16[1,3,2816]{2,1,0:T(4,128)(2,1)}, bf16[1,3,2816]{2,1,0:T(4,128)(2,1)S(1)}, u32[]{:S(2)}) copy-start(bf16[1,3,2816]{2,1,0:T(4,128)(2,1)S(1)} %copy.175) | copy-start | bytes 50692
  138.4 48.9 %all-to-all-start.2 = ((bf16[3,16,160,128]{3,2,0,1:T(8,128)(2,1)}), bf16[3,16,160,128]{3,2,0,1:T(8,128)(2,1)S(1)}, u32[]{:S(2)}, u32[]{:S(2)}) async-start(bf16[3,16,160,128]{3,2,0,1:T(8,128)(2,1)} %copy.139), calls=%async_computation.2 | async-start | bytes 3932160 | tf_op jit(solution)/shard_map/all_to_all | solution.py:203
  192.3 9.1 %copy-start.6 = (f32[256,2560]{1,0:T(8,128)S(1)}, f32[256,2560]{1,0:T(8,128)}, u32[]{:S(2)}) copy-start(f32[256,2560]{1,0:T(8,128)} %fusion.62) | copy-start | bytes 7864324
  192.3 9.1 %copy-start.7 = (f32[256,2560]{1,0:T(8,128)S(1)}, f32[256,2560]{1,0:T(8,128)}, u32[]{:S(2)}) copy-start(f32[256,2560]{1,0:T(8,128)} %copy.138) | copy-start | bytes 7864324
  192.3 9.1 %copy-start.18 = (bf16[1,3,2816]{2,1,0:T(4,128)(2,1)S(1)}, bf16[1,3,2816]{2,1,0:T(4,128)(2,1)}, u32[]{:S(2)}) copy-start(bf16[1,3,2816]{2,1,0:T(4,128)(2,1)} %copy-done.17) | copy-start | bytes 50692
  192.3 9.1 %copy-start.19 = (bf16[960,128]{1,0:T(8,128)(2,1)S(1)}, bf16[960,128]{1,0:T(8,128)(2,1)}, u32[]{:S(2)}) copy-start(bf16[960,128]{1,0:T(8,128)(2,1)} %fusion.60) | copy-start | bytes 737284
  192.3 9.2 %copy-start.51 = (bf16[256,2560]{1,0:T(8,128)(2,1)S(1)}, bf16[256,2560]{1,0:T(8,128)(2,1)}, u32[]{:S(2)}) copy-start(bf16[256,2560]{1,0:T(8,128)(2,1)} %param.12) | copy-start | bytes 3932164
  192.3 9.2 %copy-start.52 = (f32[2560]{0:T(1024)S(1)}, f32[2560]{0:T(1024)}, u32[]{:S(2)}) copy-start(f32[2560]{0:T(1024)} %convolution_reduce_fusion) | copy-start | bytes 30724
  (28 other events, 101.4 us)
Sparse Core Ops, SparseCore 0:
  52.1 140.1 all-gather.2

commit v5 on v3

--- a/solution.py
+++ b/solution.py
@@ -11,6 +11,7 @@
 INNER = 2560
 CHANNELS = 2816
 LEAD = KERNEL - 1
+LONGEST = 2048
 FINAL_VIA_ALL_TO_ALL = True
 
 f32 = jnp.float32
@@ -205,13 +206,16 @@
             (1, 0, 2),
         ).astype(f32)
 
-    own_cross = cross_dev[mine]
-    state_in = lead_state[0].reshape(HEADS, HEAD_DIM, STATE)
-    for k in range(n):
-        state_in = state_in + own_cross[k][:, None, None] * gathered_states[k].astype(
-            f32
-        ).reshape(HEADS, HEAD_DIM, STATE)
-    state_in = state_in.reshape(INNER, STATE)
+    reach = min(LONGEST // STRETCH, n)
+    back = mine - 1 - jnp.arange(reach, dtype=jnp.int32)
+    back_ok = back >= 0
+    back_c = jnp.clip(back, 0, n - 1)
+    near_w = per_head(jnp.where(back_ok[:, None], cross[mine][back_c], 0.0))
+    near_src = holder[back_c]
+    state_in = lead_state[0]
+    for i in range(reach):
+        near_state = lax.dynamic_index_in_dim(gathered_states, near_src[i], axis=0, keepdims=False)
+        state_in = state_in + near_w[i][:, None] * near_state.astype(f32)
     readout = jnp.dot(queries, state_in.astype(bf16).T, preferred_element_type=f32)
     carry_weight = jnp.exp(jnp.where((doc == prev_seq[mine])[:, None], lc, -jnp.inf))
     outputs = within + readout * per_head(carry_weight) + direct

time: 182 us -> 175 us (0.962)
  the two profiles are of different devices: /device:TPU:482 before, /device:TPU:1 now
where the time goes in v5:
time: 175 us; the launch traced here: 173 us
  local copies, waits for them, and re-layouts  37.2 us (21%)
  matrix products  35.2 us (20%)
  between operations  33.2 us (19%)
  waiting for transfers between devices  28.7 us (16%)
  other arithmetic  24.2 us (14%)
  starting transfers between devices  14.4 us (8%)
    all_to_all x1, waiting for transfers between devices, body(): lax.all_to_all(final_part.reshape(docs, n, rows_here, STATE), 'seq', 1, 1...  26.5 us
    dot_general x9, matrix products, per_head(): return jnp.matmul(x, expand, precision=lax.Precision.HIGHEST)  13.4 us
    dot_general x1, matrix products, body(): jnp.dot(queries, state_in.astype(bf16).T, preferred_element_type=f32)  8.14 us
    all_to_all x1, starting transfers between devices, body(): lax.all_to_all(jnp.broadcast_to(flat[None], (n, padded_width)), 'seq', 0,...  7.58 us
    all_to_all x1, starting transfers between devices, body(): lax.all_to_all(final_part.reshape(docs, n, rows_here, STATE), 'seq', 1, 1...  6.79 us
    dot_general x1, matrix products, body(): jnp.einsum('hts,shp->thp', mixing, scaled.reshape(STRETCH, HEADS, HEAD_DI...  5.06 us
    dot_general x1, matrix products, body(): jnp.einsum('rxk,xn->rkn', lead_mix, keys_lead.reshape(n * LEAD, STATE).as...  4.97 us
    unnamed x50, local copies, waits for them, and re-layouts  4.64 us
  transfers between devices with their start and end apart: 3, of which 2 were waited for; matrix products, arithmetic and copies ran while one was open for 35% of the time, Pallas kernels for 0%

profile of v5, /device:TPU:1, one launch (start us, length us, event | category | flops | bytes accessed | tf_op | source)
XLA Modules:
  0.0 172.9 jit_solution(15648815893952350430)
XLA Ops:
  7.3 1.3 dynamic_slice.43
  18.8 1.4 broadcast_compare_fusion
  21.2 1.1 slice_reduce_fusion.5
  23.6 2.0 %fusion.61 = f32[256,2560]{1,0:T(8,128)S(1)} fusion(s32[2560]{0:T(1024)S(1)} %add_select_fusion, bf16[256,40]{0,1:T(8,128)(2,1)} %param.13, f32[40]{0:T(128)} %param.18), kind=kOutput, calls=%fused_computation.110 | convolution fusion | flops 314757120 | bytes 2652320 | tf_op jit(solution)/shard_map/dot_general | solution.py:30
  25.7 2.7 %multiply_convert_fusion.3 = bf16[256,2816]{1,0:T(8,128)(2,1)S(1)} fusion(bf16[256,2816]{1,0:T(8,128)(2,1)S(1)} %copy-done.7, f32[2816]{0:T(1024)S(1)} %get-tuple-element.16, f32[256]{0:T(256)S(1)} %get-tuple-element.39, f32[2816]{0:T(1024)S(1)} %get-tuple-element.17, f32[256]{0:T(256)S(1)} %get-tuple-element.40, f32[2816]{0:T(1024)S(1)} %get-tuple-element.15, ...), kind=kLoop, calls=%fused_computation.38 | loop fusion | flops 14417920 | bytes 2942976 | tf_op jit(solution)/shard_map/convert_element_type | solution.py:44
  28.3 1.5 fusion.9
  29.9 1.4 convolution_convert_fusion.1
  31.3 1.6 broadcast_in_dim.161
  32.9 7.6 %all-to-all-start = ((f32[16,1,17408]{2,1,0:T(1,128)}), f32[16,1,17408]{2,1,0:T(1,128)S(1)}, u32[]{:S(2)}, u32[]{:S(2)}) async-start(f32[16,1,17408]{2,1,0:T(1,128)} %broadcast_in_dim.161), calls=%async_computation | async-start | bytes 2228224 | tf_op jit(solution)/shard_map/all_to_all | solution.py:111
  52.7 1.4 slice.272
  66.0 2.8 %fusion.59 = f32[256,2560]{1,0:T(8,128)} fusion(s32[2560]{0:T(1024)S(1)} %add_select_fusion, pred[256]{0:T(512)(128)(4,1)S(1)} %get-tuple-element.37, f32[40,2,128]{2,0,1:T(8,128)S(1)} %reduce-window.10, f32[40,2]{0,1:T(2,128)S(1)} %slice.187), kind=kOutput, calls=%fused_computation.108 | convolution fusion | flops 314695680 | bytes 2673216 | tf_op jit(solution)/shard_map/dot_general | solution.py:30
  70.9 1.9 %reshape.673 = bf16[16,6,2816]{2,1,0:T(8,128)(2,1)S(1)} reshape(bf16[16,16896]{1,0:T(8,128)(2,1)} %slice.397) | data formatting | bytes 1081344 | tf_op jit(solution)/shard_map/convert.10
  78.2 1.1 gather_fusion.3
  82.5 1.6 gather_fusion.9
  84.0 1.1 copy.151
  85.3 1.1 multiply_convert_fusion.6
  88.0 1.5 fusion.136
  89.6 3.9 %multiply_convert_fusion.1 = bf16[3,256,2560]{2,1,0:T(8,128)(2,1)S(1)} fusion(f32[256,2560]{1,0:T(8,128)S(1)} %get-tuple-element.22, s32[2560]{0:T(1024)S(1)} %add_select_fusion, f32[256,40]{0,1:T(8,128)S(1)} %get-tuple-element.31, f32[3,40]{1,0:T(4,128)S(1)} %gather_fusion, pred[3,256]{1,0:T(4,128)(4,1)S(1)} %copy-done.19), kind=kOutput, calls=%fused_computation.11 | convolution fusion | flops 947814400 | bytes 6606048 | tf_op jit(solution)/shard_map/dot_general | solution.py:30
  93.5 1.2 convolution_convert_fusion
  94.7 1.4 copy.138
  96.2 6.8 %all-to-all-start.1 = ((bf16[3,16,160,128]{3,2,0,1:T(8,128)(2,1)}), bf16[3,16,160,128]{3,2,0,1:T(8,128)(2,1)S(1)}, u32[]{:S(2)}, u32[]{:S(2)}) async-start(bf16[3,16,160,128]{3,2,0,1:T(8,128)(2,1)} %copy.138), calls=%async_computation.1 | async-start | bytes 3932160 | tf_op jit(solution)/shard_map/all_to_all | solution.py:197
  102.9 2.4 %copy.133 = bf16[256,2560]{0,1:T(8,128)(2,1)} copy(bf16[256,2560]{1,0:T(8,128)(2,1)} %get-tuple-element.23) | data formatting | bytes 2621440 | tf_op jit(solution)/shard_map/convert_element_type | solution.py:148
  105.6 5.1 %fusion = f32[40,64,256]{2,1,0:T(8,128)} fusion(bf16[256,40,64]{0,2,1:T(8,128)(2,1)} %bitcast.204, f32[40,256]{1,0:T(8,128)} %get-tuple-element.30, f32[256,256]{1,0:T(8,128)S(1)} %fusion.134, pred[256,256]{1,0:T(8,128)(4,1)} %fusion.69), kind=kOutput, calls=%fused_computation.12 | convolution fusion | flops 346030080 | bytes 4300800 | tf_op jit(solution)/shard_map/hts,shp->thp/dot_general | solution.py:177
  110.6 3.2 %copy.136 = f32[256,2560]{1,0:T(8,128)} copy(f32[256,2560]{0,1:T(8,128)} %bitcast.203) | data formatting | bytes 5242880 | tf_op jit(solution)/shard_map/reshape | solution.py:182
  114.3 1.3 fusion.11
  116.0 5.0 %convolution_bitcast_fusion = f32[4,2560,128]{2,1,0:T(8,128)S(1)} fusion(f32[16,3,2560]{2,0,1:T(8,128)S(1)} %fusion.13, f32[4,16,2560]{2,1,0:T(8,128)S(1)} %fusion.65, bf16[16,3,2816]{2,0,1:T(8,128)(2,1)} %copy-done.9), kind=kOutput, calls=%fused_computation.18 | convolution fusion | flops 755466240 | bytes 6402048 | tf_op jit(solution)/shard_map/rxk,xn->rkn/dot_general | solution.py:165
  121.0 2.3 %copy-done.6 = f32[4,2560,128]{2,1,0:T(8,128)} copy-done((f32[4,2560,128]{2,1,0:T(8,128)}, f32[4,2560,128]{2,1,0:T(8,128)S(1)}, u32[]{:S(2)}) %copy-start.6) | copy-done | bytes 5242904
  123.8 26.5 %all-to-all-done.1 = bf16[3,16,160,128]{3,2,0,1:T(8,128)(2,1)S(1)} async-done(((bf16[3,16,160,128]{3,2,0,1:T(8,128)(2,1)}), bf16[3,16,160,128]{3,2,0,1:T(8,128)(2,1)S(1)}, u32[]{:S(2)}, u32[]{:S(2)}) %all-to-all-start.1) | async-done | bytes 1966112 | tf_op jit(solution)/shard_map/all_to_all | solution.py:197
  151.3 2.2 %all-gather.3.cloned.1.call-done = bf16[40960,128]{1,0:T(8,128)(2,1)} async-done(((bf16[2560,128]{1,0:T(8,128)(2,1)}), bf16[40960,128]{1,0:T(8,128)(2,1)}) %all-gather.3.cloned.1.call-update) | async-done | bytes 10485776 | tf_op jit(solution)/shard_map/all_gather | solution.py:110
  153.5 1.1 constant_dynamic-slice_fusion
  154.7 8.1 %multiply_reduce_fusion = (f32[256]{0:T(256)S(1)}, f32[256,2560]{1,0:T(8,128)S(1)}) fusion(bf16[256,2560]{1,0:T(8,128)(2,1)} %param.12, f32[2560]{0:T(1024)} %convolution_reduce_fusion, bf16[253,2816]{1,0:T(8,128)(2,1)S(1)} %copy-done.5, bf16[3,2816]{1,0:T(4,128)(2,1)S(1)} %bitcast.208, f32[256,2560]{1,0:T(8,128)} %copy.136, f32[256,2560]{1,0:T(8,128)} %fusion.59, ...), kind=kOutput, calls=%fused_computation.44 | convolution fusion | flops 186580736 | bytes 18768928 | tf_op jit(solution)/shard_map/dot_general | solution.py:219
  163.7 1.3 multiply_convert_fusion.4
  (160 shorter events, 34.5 us)
Async XLA Ops:
  7.2 54.8 %copy-start = (f32[40]{0:T(128)S(1)}, f32[40]{0:T(128)}, u32[]{:S(2)}) copy-start(f32[40]{0:T(128)} %param.20) | copy-start | bytes 484
  7.2 18.5 %copy-start.7 = (bf16[256,2816]{1,0:T(8,128)(2,1)S(1)}, bf16[256,2816]{1,0:T(8,128)(2,1)}, u32[]{:S(2)}) copy-start(bf16[256,2816]{1,0:T(8,128)(2,1)} %param.11) | copy-start | bytes 4325380
  7.2 18.5 %copy-start.14 = (f32[2816]{0:T(1024)S(1)}, f32[2816]{0:T(1024)}, u32[]{:S(2)}) copy-start(f32[2816]{0:T(1024)} %param.17) | copy-start | bytes 33796
  7.2 146.3 %all-gather.3.cloned.1.call-start = ((), (), s32[]{:S(2)}) async-start(), calls=%async_computation.2 | async-start | bytes 11141120 | tf_op jit(solution)/shard_map/all_gather | solution.py:110
  25.6 4.2 %copy-start.2 = (f32[256,2560]{1,0:T(8,128)}, f32[256,2560]{1,0:T(8,128)S(1)}, u32[]{:S(2)}) copy-start(f32[256,2560]{1,0:T(8,128)S(1)} %fusion.61) | copy-start | bytes 7864324
  29.9 11.3 %copy-start.21 = (s32[16]{0:T(128)S(1)}, s32[16]{0:T(128)}, u32[]{:S(2)}) copy-start(s32[16]{0:T(128)} %param.15) | copy-start | bytes 196
  32.9 35.9 %all-to-all-start = ((f32[16,1,17408]{2,1,0:T(1,128)}), f32[16,1,17408]{2,1,0:T(1,128)S(1)}, u32[]{:S(2)}, u32[]{:S(2)}) async-start(f32[16,1,17408]{2,1,0:T(1,128)} %broadcast_in_dim.161), calls=%async_computation | async-start | bytes 2228224 | tf_op jit(solution)/shard_map/all_to_all | solution.py:111
  54.2 6.5 %copy-start.18 = (s32[1024]{0:T(1024)}, s32[1024]{0:T(1024)S(1)}, u32[]{:S(2)}) copy-start(s32[1024]{0:T(1024)S(1)} %pad_clamp_fusion.2) | copy-start | bytes 12292
  72.8 12.5 %copy-start.16 = (f32[16,3]{0,1:T(4,128)S(1)}, f32[16,3]{0,1:T(4,128)}, u32[]{:S(2)}) copy-start(f32[16,3]{0,1:T(4,128)} %get-tuple-element.34) | copy-start | bytes 580
  72.8 12.5 %copy-start.17 = (f32[16,3]{0,1:T(4,128)S(1)}, f32[16,3]{0,1:T(4,128)}, u32[]{:S(2)}) copy-start(f32[16,3]{0,1:T(4,128)} %get-tuple-element.35) | copy-start | bytes 580
  74.9 10.2 %copy-start.8 = (bf16[15,3,2816]{2,1,0:T(4,128)(2,1)S(1)}, bf16[15,3,2816]{2,1,0:T(4,128)(2,1)}, u32[]{:S(2)}) copy-start(bf16[15,3,2816]{2,1,0:T(4,128)(2,1)} %slice.268) | copy-start | bytes 760324
  80.1 7.9 %copy-start.3 = (f32[256,2560]{1,0:T(8,128)S(1)}, f32[256,2560]{1,0:T(8,128)}, u32[]{:S(2)}) copy-start(f32[256,2560]{1,0:T(8,128)} %copy-done.2) | copy-start | bytes 7864324
  84.0 4.0 %copy-start.4 = (bf16[253,2816]{1,0:T(8,128)(2,1)S(1)}, bf16[253,2816]{1,0:T(8,128)(2,1)}, u32[]{:S(2)}) copy-start(bf16[253,2816]{1,0:T(8,128)(2,1)} %slice.272) | copy-start | bytes 4274692
  86.4 0.7 copy-start.9
  88.0 1.6 copy-start.19
  96.1 9.2 %copy-start.5 = (bf16[253,2816]{1,0:T(8,128)(2,1)S(1)}, bf16[253,2816]{1,0:T(8,128)(2,1)}, u32[]{:S(2)}) copy-start(bf16[253,2816]{1,0:T(8,128)(2,1)} %slice.272) | copy-start | bytes 4274692
  96.2 54.2 %all-to-all-start.1 = ((bf16[3,16,160,128]{3,2,0,1:T(8,128)(2,1)}), bf16[3,16,160,128]{3,2,0,1:T(8,128)(2,1)S(1)}, u32[]{:S(2)}, u32[]{:S(2)}) async-start(bf16[3,16,160,128]{3,2,0,1:T(8,128)(2,1)} %copy.138), calls=%async_computation.1 | async-start | bytes 3932160 | tf_op jit(solution)/shard_map/all_to_all | solution.py:197
  110.6 3.7 %copy-start.12 = (f32[16,3,40]{2,1,0:T(4,128)S(1)}, f32[16,3,40]{2,1,0:T(4,128)}, u32[]{:S(2)}) copy-start(f32[16,3,40]{2,1,0:T(4,128)} %reshape.668) | copy-start | bytes 23044
  110.6 5.0 %copy-start.13 = (f32[16,3,40]{2,1,0:T(4,128)S(1)}, f32[16,3,40]{2,1,0:T(4,128)}, u32[]{:S(2)}) copy-start(f32[16,3,40]{2,1,0:T(4,128)} %reshape.669) | copy-start | bytes 23044
  121.0 2.4 %copy-start.6 = (f32[4,2560,128]{2,1,0:T(8,128)}, f32[4,2560,128]{2,1,0:T(8,128)S(1)}, u32[]{:S(2)}) copy-start(f32[4,2560,128]{2,1,0:T(8,128)S(1)} %convolution_bitcast_fusion) | copy-start | bytes 15728644
  121.0 2.4 %copy-start.20 = (f32[8,40]{1,0:T(8,128)S(1)}, f32[8,40]{1,0:T(8,128)}, u32[]{:S(2)}) copy-start(f32[8,40]{1,0:T(8,128)} %gather_fusion.3) | copy-start | bytes 3844
  121.0 2.4 %copy-start.22 = (pred[8]{0:T(512)(128)(4,1)S(1)}, pred[8]{0:T(512)(128)(4,1)}, u32[]{:S(2)}) copy-start(pred[8]{0:T(512)(128)(4,1)} %subtract_compare_fusion) | copy-start | bytes 28
  154.6 8.2 %copy-start.11 = (f32[160,3,16]{2,1,0:T(4,128)S(1)}, f32[160,3,16]{2,1,0:T(4,128)}, u32[]{:S(2)}) copy-start(f32[160,3,16]{2,1,0:T(4,128)} %gather_fusion.9) | copy-start | bytes 92164
  154.6 9.0 %copy-start.15 = (f32[2560]{0:T(1024)S(1)}, f32[2560]{0:T(1024)}, u32[]{:S(2)}) copy-start(f32[2560]{0:T(1024)} %param.21) | copy-start | bytes 30724
  162.8 2.2 %slice-start = ((f32[4,2560,128]{2,1,0:T(8,128)}), f32[3,2560,128]{2,1,0:T(8,128)S(1)}, s32[]{:S(2)}) async-start(f32[4,2560,128]{2,1,0:T(8,128)} %copy-done.6), calls=%async_computation.3 | async-start | bytes 7864320 | tf_op jit(solution)/shard_map/slice | solution.py:233
  162.8 2.4 %copy-start.10 = (f32[3,160,128]{2,1,0:T(8,128)S(1)}, f32[3,160,128]{2,1,0:T(8,128)}, u32[]{:S(2)}) copy-start(f32[3,160,128]{2,1,0:T(8,128)} %convert_reduce_fusion) | copy-start | bytes 737284
  162.8 3.2 %copy-start.1 = (f32[40]{0:T(128)S(1)}, f32[40]{0:T(128)}, u32[]{:S(2)}) copy-start(f32[40]{0:T(128)} %param.20) | copy-start | bytes 484
Sparse Core Ops, SparseCore 0:
  31.4 122.0 all-gather.2

commit v6 on v5

--- a/solution.py
+++ b/solution.py
@@ -85,20 +85,25 @@
     weighted_local = (scaled_local.astype(f32) * per_head(weight_end)).astype(bf16)
     state_part = jnp.dot(weighted_local.T, keys_local, preferred_element_type=f32)
 
+    edge_raw = jnp.concatenate([mixer_in[:LEAD], mixer_in[STRETCH - LEAD :]], 0)
+    state_send, lc_b, step_b, edge_b = lax.optimization_barrier(
+        (state_part.astype(bf16), lc, step, edge_raw)
+    )
+    gathered_states = lax.all_gather(state_send, "seq", axis=0, tiled=False)
+    total_b = lc_b[-1]
     doc_last = ends - 1
     doc_owner = doc_last // STRETCH
     doc_at = doc_last - doc_owner * STRETCH
     lc_at_end = jnp.where(
-        (doc_owner == mine)[:, None], lc[jnp.clip(doc_at, 0, STRETCH - 1)], 0.0
+        (doc_owner == mine)[:, None], lc_b[jnp.clip(doc_at, 0, STRETCH - 1)], 0.0
     )
     w_lead = jnp.where(
-        (doc[:LEAD] == end_doc_mine)[:, None], jnp.exp(total[None, :] - lc[:LEAD]), 0.0
-    )
-    edge_rows = jnp.concatenate([mixer_in[:LEAD], mixer_in[STRETCH - LEAD :]], 0).astype(f32)
+        (doc[:LEAD] == end_doc_mine)[:, None], jnp.exp(total_b[None, :] - lc_b[:LEAD]), 0.0
+    )
     pieces = [
-        edge_rows.reshape(-1),
-        total,
-        step[:LEAD].reshape(-1),
+        edge_b.astype(f32).reshape(-1),
+        total_b,
+        step_b[:LEAD].reshape(-1),
         w_lead.reshape(-1),
         lc_at_end.reshape(-1),
     ]
@@ -106,8 +111,6 @@
     width = flat.shape[0]
     padded_width = -(-width // 128) * 128
     flat = jnp.pad(flat, (0, padded_width - width))
-    flat, state_send = lax.optimization_barrier((flat, state_part.astype(bf16)))
-    gathered_states = lax.all_gather(state_send, "seq", axis=0, tiled=False)
     small = lax.all_to_all(
         jnp.broadcast_to(flat[None], (n, padded_width)), "seq", 0, 0, tiled=True
     )

time: 175 us -> 179 us (1.023)
  other arithmetic: 24.2 us -> 27.5 us
    convert_element_type x2, other arithmetic: 3.76 us -> 6.98 us  [conv_rows(): return jax.nn.silu(accum).astype(bf16)]
  transfers between devices with their start and end apart: 3 -> 3, of which waited for: 2 -> 2; matrix products, arithmetic and copies ran while one was open for 35% -> 36% of each run, Pallas kernels for 0% -> 0%
where the time goes in v6:
time: 179 us; the launch traced here: 176 us
  local copies, waits for them, and re-layouts  38.1 us (21%)
  matrix products  35.6 us (20%)
  between operations  33.1 us (18%)
  waiting for transfers between devices  27.8 us (16%)
  other arithmetic  27.5 us (15%)
  starting transfers between devices  14.4 us (8%)
    all_to_all x1, waiting for transfers between devices, body(): lax.all_to_all(final_part.reshape(docs, n, rows_here, STATE), 'seq', 1, 1...  25.9 us
    dot_general x9, matrix products, per_head(): return jnp.matmul(x, expand, precision=lax.Precision.HIGHEST)  13.4 us
    dot_general x1, matrix products, body(): jnp.dot(queries, state_in.astype(bf16).T, preferred_element_type=f32)  8.46 us
    all_to_all x1, starting transfers between devices, body(): lax.all_to_all(jnp.broadcast_to(flat[None], (n, padded_width)), 'seq', 0,...  7.58 us
    convert_element_type x2, other arithmetic, conv_rows(): return jax.nn.silu(accum).astype(bf16)  6.98 us
    all_to_all x1, starting transfers between devices, body(): lax.all_to_all(final_part.reshape(docs, n, rows_here, STATE), 'seq', 1, 1...  6.8 us
    dot_general x1, matrix products, body(): jnp.einsum('hts,shp->thp', mixing, scaled.reshape(STRETCH, HEADS, HEAD_DI...  5.06 us
    dot_general x1, matrix products, body(): jnp.einsum('rxk,xn->rkn', lead_mix, keys_lead.reshape(n * LEAD, STATE).as...  4.97 us
  transfers between devices with their start and end apart: 3, of which 2 were waited for; matrix products, arithmetic and copies ran while one was open for 36% of the time, Pallas kernels for 0%

profile of v6, /device:TPU:1, one launch (start us, length us, event | category | flops | bytes accessed | tf_op | source)
XLA Modules:
  0.0 176.5 jit_solution(3379650974226223013)
XLA Ops:
  7.2 1.2 dynamic_slice.43
  14.2 1.1 slice_reduce_fusion.6
  17.8 2.0 %fusion.61 = f32[256,2560]{1,0:T(8,128)S(1)} fusion(s32[2560]{0:T(1024)S(1)} %add_select_fusion, bf16[256,40]{0,1:T(8,128)(2,1)} %param.13, f32[40]{0:T(128)} %param.18), kind=kOutput, calls=%fused_computation.111 | convolution fusion | flops 314757120 | bytes 2652320 | tf_op jit(solution)/shard_map/dot_general | solution.py:30
  21.3 1.4 broadcast_compare_fusion
  22.6 5.9 %multiply_convert_fusion.3 = bf16[256,2816]{1,0:T(8,128)(2,1)S(1)} fusion(bf16[256,2816]{1,0:T(8,128)(2,1)} %param.11, f32[2816]{0:T(1024)S(1)} %get-tuple-element.20, f32[256]{0:T(256)S(1)} %get-tuple-element.43, f32[2816]{0:T(1024)S(1)} %get-tuple-element.21, f32[256]{0:T(256)S(1)} %get-tuple-element.44, f32[2816]{0:T(1024)S(1)} %get-tuple-element.19, ...), kind=kLoop, calls=%fused_computation.39 | loop fusion | flops 14417920 | bytes 2942976 | tf_op jit(solution)/shard_map/convert_element_type | solution.py:44
  28.5 1.5 fusion.9
  30.1 1.4 convolution_convert_fusion.1
  34.8 1.6 broadcast_in_dim.161
  36.3 7.6 %all-to-all-start = ((f32[16,1,17408]{2,1,0:T(1,128)}), f32[16,1,17408]{2,1,0:T(1,128)S(1)}, u32[]{:S(2)}, u32[]{:S(2)}) async-start(f32[16,1,17408]{2,1,0:T(1,128)} %broadcast_in_dim.161), calls=%async_computation | async-start | bytes 2228224 | tf_op jit(solution)/shard_map/all_to_all | solution.py:114
  56.3 1.4 slice.276
  70.1 2.8 %fusion.59 = f32[256,2560]{1,0:T(8,128)} fusion(s32[2560]{0:T(1024)S(1)} %add_select_fusion, pred[256]{0:T(512)(128)(4,1)S(1)} %get-tuple-element.41, f32[40,2,128]{2,0,1:T(8,128)S(1)} %reduce-window.11, f32[40,2]{0,1:T(2,128)S(1)} %slice.199), kind=kOutput, calls=%fused_computation.109 | convolution fusion | flops 314695680 | bytes 2673216 | tf_op jit(solution)/shard_map/dot_general | solution.py:30
  75.0 1.9 %reshape.678 = bf16[16,6,2816]{2,1,0:T(8,128)(2,1)S(1)} reshape(bf16[16,16896]{1,0:T(8,128)(2,1)} %slice.398) | data formatting | bytes 1081344 | tf_op jit(solution)/shard_map/convert.10
  82.3 1.1 gather_fusion.3
  86.6 1.6 gather_fusion.10
  88.1 1.1 copy.153
  89.4 1.1 multiply_convert_fusion.6
  91.5 1.5 fusion.134
  93.1 3.9 %multiply_convert_fusion.1 = bf16[3,256,2560]{2,1,0:T(8,128)(2,1)S(1)} fusion(f32[256,2560]{1,0:T(8,128)S(1)} %get-tuple-element.26, s32[2560]{0:T(1024)S(1)} %add_select_fusion, f32[256,40]{0,1:T(8,128)S(1)} %get-tuple-element.7, f32[3,40]{1,0:T(4,128)S(1)} %gather_fusion.5, pred[3,256]{1,0:T(4,128)(4,1)S(1)} %copy-done.19), kind=kOutput, calls=%fused_computation.12 | convolution fusion | flops 947814400 | bytes 6606048 | tf_op jit(solution)/shard_map/dot_general | solution.py:30
  97.0 1.2 convolution_convert_fusion
  98.2 1.4 copy.140
  99.7 6.8 %all-to-all-start.1 = ((bf16[3,16,160,128]{3,2,0,1:T(8,128)(2,1)}), bf16[3,16,160,128]{3,2,0,1:T(8,128)(2,1)S(1)}, u32[]{:S(2)}, u32[]{:S(2)}) async-start(bf16[3,16,160,128]{3,2,0,1:T(8,128)(2,1)} %copy.140), calls=%async_computation.1 | async-start | bytes 3932160 | tf_op jit(solution)/shard_map/all_to_all | solution.py:200
  106.5 2.4 %copy.134 = bf16[256,2560]{0,1:T(8,128)(2,1)} copy(bf16[256,2560]{1,0:T(8,128)(2,1)} %get-tuple-element.27) | data formatting | bytes 2621440 | tf_op jit(solution)/shard_map/convert_element_type | solution.py:151
  109.1 5.1 %fusion = f32[40,64,256]{2,1,0:T(8,128)} fusion(bf16[256,40,64]{0,2,1:T(8,128)(2,1)} %bitcast.204, f32[40,256]{1,0:T(8,128)} %get-tuple-element.34, f32[256,256]{1,0:T(8,128)S(1)} %fusion.132, pred[256,256]{1,0:T(8,128)(4,1)} %fusion.69), kind=kOutput, calls=%fused_computation.13 | convolution fusion | flops 346030080 | bytes 4300800 | tf_op jit(solution)/shard_map/hts,shp->thp/dot_general | solution.py:180
  114.2 3.2 %copy.137 = f32[256,2560]{1,0:T(8,128)} copy(f32[256,2560]{0,1:T(8,128)} %bitcast.203) | data formatting | bytes 5242880 | tf_op jit(solution)/shard_map/reshape | solution.py:185
  117.8 1.3 fusion.11
  119.5 5.0 %convolution_bitcast_fusion = f32[4,2560,128]{2,1,0:T(8,128)S(1)} fusion(f32[16,3,2560]{2,0,1:T(8,128)S(1)} %fusion.13, f32[4,16,2560]{2,1,0:T(8,128)S(1)} %fusion.65, bf16[16,3,2816]{2,0,1:T(8,128)(2,1)} %copy-done.10), kind=kOutput, calls=%fused_computation.19 | convolution fusion | flops 755466240 | bytes 6402048 | tf_op jit(solution)/shard_map/rxk,xn->rkn/dot_general | solution.py:168
  124.5 2.3 %copy-done.6 = f32[4,2560,128]{2,1,0:T(8,128)} copy-done((f32[4,2560,128]{2,1,0:T(8,128)}, f32[4,2560,128]{2,1,0:T(8,128)S(1)}, u32[]{:S(2)}) %copy-start.6) | copy-done | bytes 5242904
  128.0 25.9 %all-to-all-done.1 = bf16[3,16,160,128]{3,2,0,1:T(8,128)(2,1)S(1)} async-done(((bf16[3,16,160,128]{3,2,0,1:T(8,128)(2,1)}), bf16[3,16,160,128]{3,2,0,1:T(8,128)(2,1)S(1)}, u32[]{:S(2)}, u32[]{:S(2)}) %all-to-all-start.1) | async-done | bytes 1966112 | tf_op jit(solution)/shard_map/all_to_all | solution.py:200
  154.8 1.9 %all-gather.3.cloned.1.call-done = bf16[40960,128]{1,0:T(8,128)(2,1)} async-done(((bf16[2560,128]{1,0:T(8,128)(2,1)}), bf16[40960,128]{1,0:T(8,128)(2,1)}) %all-gather.3.cloned.1.call-update) | async-done | bytes 10485776 | tf_op jit(solution)/shard_map/all_gather | solution.py:92
  156.7 1.1 constant_dynamic-slice_fusion
  157.9 8.5 %multiply_reduce_fusion = (f32[256]{0:T(256)S(1)}, f32[256,2560]{1,0:T(8,128)S(1)}) fusion(bf16[256,2560]{1,0:T(8,128)(2,1)} %param.12, f32[2560]{0:T(1024)} %convolution_reduce_fusion, bf16[253,2816]{1,0:T(8,128)(2,1)S(1)} %copy-done.5, bf16[3,2816]{1,0:T(4,128)(2,1)S(1)} %bitcast.208, f32[256,2560]{1,0:T(8,128)} %copy.137, f32[256,2560]{1,0:T(8,128)} %fusion.59, ...), kind=kOutput, calls=%fused_computation.45 | convolution fusion | flops 186580736 | bytes 18768928 | tf_op jit(solution)/shard_map/dot_general | solution.py:222
  167.2 1.3 multiply_convert_fusion.4
  (163 shorter events, 35.6 us)
Async XLA Ops:
  7.2 58.9 %copy-start = (f32[40]{0:T(128)S(1)}, f32[40]{0:T(128)}, u32[]{:S(2)}) copy-start(f32[40]{0:T(128)} %param.20) | copy-start | bytes 484
  7.2 15.4 %copy-start.15 = (f32[2816]{0:T(1024)S(1)}, f32[2816]{0:T(1024)}, u32[]{:S(2)}) copy-start(f32[2816]{0:T(1024)} %param.17) | copy-start | bytes 33796
  7.2 149.5 %all-gather.3.cloned.1.call-start = ((), (), s32[]{:S(2)}) async-start(), calls=%async_computation.2 | async-start | bytes 11141120 | tf_op jit(solution)/shard_map/all_gather | solution.py:92
  19.9 10.2 %copy-start.2 = (f32[256,2560]{1,0:T(8,128)}, f32[256,2560]{1,0:T(8,128)S(1)}, u32[]{:S(2)}) copy-start(f32[256,2560]{1,0:T(8,128)S(1)} %fusion.61) | copy-start | bytes 7864324
  28.5 1.6 copy-start.7
  31.5 13.1 %copy-start.21 = (s32[16]{0:T(128)S(1)}, s32[16]{0:T(128)}, u32[]{:S(2)}) copy-start(s32[16]{0:T(128)} %param.15) | copy-start | bytes 196
  31.6 24.7 %copy-start.8 = (bf16[256,2816]{1,0:T(8,128)(2,1)S(1)}, bf16[256,2816]{1,0:T(8,128)(2,1)}, u32[]{:S(2)}) copy-start(bf16[256,2816]{1,0:T(8,128)(2,1)} %copy-done.7) | copy-start | bytes 4325380
  36.3 36.5 %all-to-all-start = ((f32[16,1,17408]{2,1,0:T(1,128)}), f32[16,1,17408]{2,1,0:T(1,128)S(1)}, u32[]{:S(2)}, u32[]{:S(2)}) async-start(f32[16,1,17408]{2,1,0:T(1,128)} %broadcast_in_dim.161), calls=%async_computation | async-start | bytes 2228224 | tf_op jit(solution)/shard_map/all_to_all | solution.py:114
  57.7 11.6 %copy-start.18 = (s32[1024]{0:T(1024)}, s32[1024]{0:T(1024)S(1)}, u32[]{:S(2)}) copy-start(s32[1024]{0:T(1024)S(1)} %pad_clamp_fusion.2) | copy-start | bytes 12292
  76.9 12.5 %copy-start.17 = (f32[16,3]{0,1:T(4,128)S(1)}, f32[16,3]{0,1:T(4,128)}, u32[]{:S(2)}) copy-start(f32[16,3]{0,1:T(4,128)} %get-tuple-element.39) | copy-start | bytes 580
  79.0 10.2 %copy-start.9 = (bf16[15,3,2816]{2,1,0:T(4,128)(2,1)S(1)}, bf16[15,3,2816]{2,1,0:T(4,128)(2,1)}, u32[]{:S(2)}) copy-start(bf16[15,3,2816]{2,1,0:T(4,128)(2,1)} %slice.272) | copy-start | bytes 760324
  84.1 7.4 %copy-start.3 = (f32[256,2560]{1,0:T(8,128)S(1)}, f32[256,2560]{1,0:T(8,128)}, u32[]{:S(2)}) copy-start(f32[256,2560]{1,0:T(8,128)} %copy-done.2) | copy-start | bytes 7864324
  88.1 3.4 %copy-start.4 = (bf16[253,2816]{1,0:T(8,128)(2,1)S(1)}, bf16[253,2816]{1,0:T(8,128)(2,1)}, u32[]{:S(2)}) copy-start(bf16[253,2816]{1,0:T(8,128)(2,1)} %slice.276) | copy-start | bytes 4274692
  90.5 2.6 %copy-start.10 = (bf16[16,3,2816]{2,0,1:T(8,128)(2,1)}, bf16[16,3,2816]{2,0,1:T(8,128)(2,1)S(1)}, u32[]{:S(2)}) copy-start(bf16[16,3,2816]{2,0,1:T(8,128)(2,1)S(1)} %multiply_convert_fusion.6) | copy-start | bytes 811012
  91.5 1.6 copy-start.19
  99.7 9.3 %copy-start.5 = (bf16[253,2816]{1,0:T(8,128)(2,1)S(1)}, bf16[253,2816]{1,0:T(8,128)(2,1)}, u32[]{:S(2)}) copy-start(bf16[253,2816]{1,0:T(8,128)(2,1)} %slice.276) | copy-start | bytes 4274692
  99.7 54.2 %all-to-all-start.1 = ((bf16[3,16,160,128]{3,2,0,1:T(8,128)(2,1)}), bf16[3,16,160,128]{3,2,0,1:T(8,128)(2,1)S(1)}, u32[]{:S(2)}, u32[]{:S(2)}) async-start(bf16[3,16,160,128]{3,2,0,1:T(8,128)(2,1)} %copy.140), calls=%async_computation.1 | async-start | bytes 3932160 | tf_op jit(solution)/shard_map/all_to_all | solution.py:200
  114.2 3.7 %copy-start.13 = (f32[16,3,40]{2,1,0:T(4,128)S(1)}, f32[16,3,40]{2,1,0:T(4,128)}, u32[]{:S(2)}) copy-start(f32[16,3,40]{2,1,0:T(4,128)} %reshape.672) | copy-start | bytes 23044
  114.2 5.0 %copy-start.14 = (f32[16,3,40]{2,1,0:T(4,128)S(1)}, f32[16,3,40]{2,1,0:T(4,128)}, u32[]{:S(2)}) copy-start(f32[16,3,40]{2,1,0:T(4,128)} %reshape.673) | copy-start | bytes 23044
  124.5 2.4 %copy-start.6 = (f32[4,2560,128]{2,1,0:T(8,128)}, f32[4,2560,128]{2,1,0:T(8,128)S(1)}, u32[]{:S(2)}) copy-start(f32[4,2560,128]{2,1,0:T(8,128)S(1)} %convolution_bitcast_fusion) | copy-start | bytes 15728644
  124.5 2.4 %copy-start.20 = (f32[8,40]{1,0:T(8,128)S(1)}, f32[8,40]{1,0:T(8,128)}, u32[]{:S(2)}) copy-start(f32[8,40]{1,0:T(8,128)} %gather_fusion.3) | copy-start | bytes 3844
  124.5 2.4 %copy-start.22 = (pred[8]{0:T(512)(128)(4,1)S(1)}, pred[8]{0:T(512)(128)(4,1)}, u32[]{:S(2)}) copy-start(pred[8]{0:T(512)(128)(4,1)} %subtract_compare_fusion) | copy-start | bytes 28
  157.9 8.5 %copy-start.12 = (f32[160,3,16]{2,1,0:T(4,128)S(1)}, f32[160,3,16]{2,1,0:T(4,128)}, u32[]{:S(2)}) copy-start(f32[160,3,16]{2,1,0:T(4,128)} %gather_fusion.10) | copy-start | bytes 92164
  157.9 9.3 %copy-start.16 = (f32[2560]{0:T(1024)S(1)}, f32[2560]{0:T(1024)}, u32[]{:S(2)}) copy-start(f32[2560]{0:T(1024)} %param.21) | copy-start | bytes 30724
  166.4 2.2 %slice-start = ((f32[4,2560,128]{2,1,0:T(8,128)}), f32[3,2560,128]{2,1,0:T(8,128)S(1)}, s32[]{:S(2)}) async-start(f32[4,2560,128]{2,1,0:T(8,128)} %copy-done.6), calls=%async_computation.3 | async-start | bytes 7864320 | tf_op jit(solution)/shard_map/slice | solution.py:236
  166.4 2.4 %copy-start.11 = (f32[3,160,128]{2,1,0:T(8,128)S(1)}, f32[3,160,128]{2,1,0:T(8,128)}, u32[]{:S(2)}) copy-start(f32[3,160,128]{2,1,0:T(8,128)} %convert_reduce_fusion) | copy-start | bytes 737284
  166.4 3.2 %copy-start.1 = (f32[40]{0:T(128)S(1)}, f32[40]{0:T(128)}, u32[]{:S(2)}) copy-start(f32[40]{0:T(128)} %param.20) | copy-start | bytes 484
Sparse Core Ops, SparseCore 0:
  31.7 125.0 all-gather.2
